TPU v7x, 32 devices: a whole 2x2x4 slice. The times are simulated.
32 devices in a mesh: job: 2 (over x), space: 4 (over y, core), arc: 4 (over z).
Axes of the slice: x: 2, y: 2, z: 4, core: 2. Of those that a mesh axis runs over, the one named last changes fastest.
Arguments:
- saved_velocity_trajectory: bfloat16 [64, 3, 8, 128, 128], P(('job', 'arc'), None, 'space'), parts along dimension 0, may hold values from -4 to 4
- saved_warmth_trajectory: bfloat16 [64, 8, 128, 128], P(('job', 'arc'), 'space'), parts along dimension 0, may hold values from -5 to 5
- control_porosity: float32 [16, 128, 128], P(('job', 'space')), parts along dimension 0, may hold values from 0.05 to 1
- control_volume_flag: int32 [16, 128, 128], P(('job', 'space')), parts along dimension 0, may hold values 0 or 1
- entrance_face_flag: int32 [256, 128], P('job'), parts along dimension 0, may hold values 0 or 1
Outputs:
- gradient: float32 [16, 128, 128], P(('job', 'space'), 'arc'), parts along dimension 0
- entry_adjoint: float32 [8, 4, 8, 128, 128], P(('job', 'arc'), None, 'space'), parts along dimension 0
There are 2 independent parts, one for each index of `job`. A program takes and returns all parts, laid end to end along the dimension named above; each array names one. Nothing has to cross between parts.
All inputs are finite; a program needn't handle non-finite values. No bound on the sum of `control_volume_flag` on one device may be relied on, other than what follows from the above.
Results may differ from a plain program's by a relative error of at most 0.0003.
Values may be sent and summed in bfloat16 or wider, within the bound.
No kernel may reach another device: no remote copies, remote signals or barrier semaphores. Data moves between devices by JAX's collectives and lax.ppermute only.
A program may use at most 64 MiB of HBM per device.

v0:
```python
import jax
import jax.numpy as jnp
from jax import lax
from jax.sharding import PartitionSpec as P


def padded(cells, sides, width):
    for axis, dim in sides:
        count = lax.axis_size(axis)
        ends = count - 1
        head = lax.slice_in_dim(cells, 0, width, axis=dim)
        tail = lax.slice_in_dim(cells, cells.shape[dim] - width, cells.shape[dim], axis=dim)
        cells = jnp.concatenate(
            [
                lax.ppermute(tail, axis, [(i, (i + 1) % count) for i in range(ends)]),
                cells,
                lax.ppermute(head, axis, [((i + 1) % count, i) for i in range(ends)]),
            ],
            axis=dim,
        )
    return cells


def passed_along(value, axis, steps):
    count = lax.axis_size(axis)
    pairs = [(source, (source + steps) % count) for source in range(count)]
    return lax.ppermute(value, axis, pairs)


def laplace(ext):
    mid = ext[..., 1:-1, 1:-1, 1:-1]
    total = ext[..., 2:, 1:-1, 1:-1] + ext[..., :-2, 1:-1, 1:-1]
    total = total + ext[..., 1:-1, 2:, 1:-1] + ext[..., 1:-1, :-2, 1:-1]
    total = total + ext[..., 1:-1, 1:-1, 2:] + ext[..., 1:-1, 1:-1, :-2]
    return total - 6.0 * mid


def slopes(ext):
    return (
        0.5 * (ext[..., 2:, 1:-1, 1:-1] - ext[..., :-2, 1:-1, 1:-1]),
        0.5 * (ext[..., 1:-1, 2:, 1:-1] - ext[..., 1:-1, :-2, 1:-1]),
        0.5 * (ext[..., 1:-1, 1:-1, 2:] - ext[..., 1:-1, 1:-1, :-2]),
    )


def pad_sides(field, operating_variant):
    widths = [(0, 0)] * (field.ndim - 2) + [(1, 1), (1, 1)]
    return jnp.pad(field, widths, mode=operating_variant)


def adjoint_update(
    adj,
    ext_a,
    ext_b,
    padded_thermal_field,
    speed,
    alpha,
    porosity_sensitivity,
    solid,
    quadrature_factor,
):
    a_now = adj[:3]
    current_adjoint_vector = adj[3]
    grad_b = slopes(ext_b)
    grad_a = slopes(ext_a)
    grad_t = slopes(padded_thermal_field)
    carry_b = speed[0] * grad_b[0] + speed[1] * grad_b[1] + speed[2] * grad_b[2]
    carry_a = speed[0:1] * grad_a[0] + speed[1:2] * grad_a[1] + speed[2:3] * grad_a[2]
    thermal_current_field = padded_thermal_field[1:-1, 1:-1, 1:-1]
    grad_stack = jnp.stack(grad_t)
    new_a = a_now + 0.1 * (
        1.2 * laplace(ext_a) + carry_a - alpha * a_now - current_adjoint_vector * grad_stack
    )
    new_b = current_adjoint_vector + 0.1 * (
        1.2 * laplace(ext_b) + carry_b - 2.0 * solid * current_adjoint_vector + 2.0 * solid
    )
    common_divisor_lcm_like = jnp.sum(a_now * speed, axis=0)
    summand_contribution = (
        0.1
        * quadrature_factor
        * (
            porosity_sensitivity * common_divisor_lcm_like
            + 2.0 * (current_adjoint_vector - 1.0) * thermal_current_field
        )
    )
    return (jnp.concatenate([new_a, new_b[None]], axis=0), summand_contribution)


def body(
    saved_velocity_trajectory,
    saved_warmth_trajectory,
    control_porosity,
    control_volume_flag,
    entrance_face_flag,
):
    quadrature_factor = control_volume_flag.astype(jnp.float32)
    gamma = jnp.where(control_volume_flag == 1, control_porosity, jnp.float32(0.0))
    solid = 1.0 - gamma
    alpha = 3.0 * 0.1 * solid / (0.1 + gamma)
    porosity_sensitivity = -3.0 * 0.1 * 1.1 / ((0.1 + gamma) * (0.1 + gamma))
    leading_plane = lax.axis_index("space") == 0
    trailing_plane = lax.axis_index("space") == lax.axis_size("space") - 1
    device_instant_total = saved_warmth_trajectory.shape[0]
    cycle_ext = padded(saved_warmth_trajectory, (("space", 1),), 1)

    def closing_thermal_value(thermal_current_field, with_halo_padding):
        floor_limit = jnp.where(leading_plane, thermal_current_field[0], with_halo_padding[0])
        ceiling_bound = jnp.where(trailing_plane, thermal_current_field[-1], with_halo_padding[-1])
        return pad_sides(
            jnp.concatenate(
                [floor_limit[None], thermal_current_field, ceiling_bound[None]], axis=0
            ),
            "edge",
        )

    def one_step(adj, interior_block):
        speed = saved_velocity_trajectory[interior_block].astype(jnp.float32)
        thermal_current_field = saved_warmth_trajectory[interior_block].astype(jnp.float32)
        with_halo_padding = padded(adj, (("space", 1),), 1)
        thermal_halo_values = cycle_ext[interior_block].astype(jnp.float32)
        complete_thermal_field = jnp.concatenate(
            [thermal_halo_values[:1], thermal_current_field, thermal_halo_values[-1:]], axis=0
        )
        padded_thermal_field = closing_thermal_value(thermal_current_field, complete_thermal_field)
        ext_a = pad_sides(with_halo_padding[:3], "constant")
        current_adjoint_vector = adj[3]
        floor_limit = jnp.where(
            leading_plane,
            jnp.where(entrance_face_flag == 1, jnp.float32(0.0), current_adjoint_vector[0]),
            with_halo_padding[3, 0],
        )
        ceiling_bound = jnp.where(
            trailing_plane, current_adjoint_vector[-1], with_halo_padding[3, -1]
        )
        ext_b = pad_sides(
            jnp.concatenate(
                [floor_limit[None], current_adjoint_vector, ceiling_bound[None]], axis=0
            ),
            "edge",
        )
        return adjoint_update(
            adj,
            ext_a,
            ext_b,
            padded_thermal_field,
            speed,
            alpha,
            porosity_sensitivity,
            solid,
            quadrature_factor,
        )

    grid_shape = (4,) + control_porosity.shape
    adj = jnp.zeros(grid_shape, jnp.float32)
    for interior_block in range(device_instant_total - 1, -1, -1):
        adj, unused = one_step(adj, interior_block)
    adj = passed_along(adj, "arc", -1)
    partial_sum = jnp.zeros(control_porosity.shape, jnp.float32)
    for interior_block in range(device_instant_total - 1, -1, -1):
        adj, summand_contribution = one_step(adj, interior_block)
        partial_sum = partial_sum + summand_contribution
    summed = lax.psum(partial_sum, "arc")
    share = summed.shape[1] // lax.axis_size("arc")
    gradient = lax.dynamic_slice_in_dim(summed, lax.axis_index("arc") * share, share, 1)
    return (gradient, adj[None])


def solution(mesh):
    return jax.shard_map(
        body,
        mesh=mesh,
        in_specs=(
            P(("job", "arc"), None, "space", None, None),
            P(("job", "arc"), "space", None, None),
            P(("job", "space"), None, None),
            P(("job", "space"), None, None),
            P("job", None),
        ),
        out_specs=(P(("job", "space"), "arc", None), P(("job", "arc"), None, "space", None, None)),
        check_vma=False,
    )
```

profile of v0, /device:TPU:0, one launch (start us, length us, event | category | flops | bytes accessed | tf_op | source)
XLA Modules:
  0.0 265.9 jit_solution(15857158346192255144)
XLA Ops:
  8.0 1.4 collective-permute-start
  9.4 3.8 %collective-permute-start.1 = (f32[4,1,128,128]{3,2,1,0:T(8,128)}, f32[4,1,128,128]{3,2,1,0:T(8,128)}, u32[]{:S(2)}, u32[]{:S(2)}) collective-permute-start(f32[4,1,128,128]{3,2,1,0:T(8,128)} %broadcast.302), channel_id=1, source_target_pairs={{0,4},{4,8},{8,12},{1,5},{5,9},{9,13},{2,6},{6,10},{10,14},{3,7},{... | collective-permute-start | bytes 786440 | tf_op jit(solution)/shard_map/ppermute | solution.py:15
  13.1 1.9 fusion.209
  15.0 4.5 %collective-permute-start.2 = (bf16[8,1,128,128]{3,2,1,0:T(8,128)(2,1)}, bf16[8,1,128,128]{3,2,1,0:T(8,128)(2,1)}, u32[]{:S(2)}, u32[]{:S(2)}) collective-permute-start(bf16[8,1,128,128]{3,2,1,0:T(8,128)(2,1)} %get-tuple-element.84), channel_id=1, source_target_pairs={{0,4},{4,8},{8,12},{1,5},{5,9},{9,13},{2,6},{6,10},{10,14},{3,7},{... | collective-permute-start | bytes 786440 | tf_op jit(solution)/shard_map/ppermute | solution.py:15
  19.5 1.3 collective-permute-start.3
  20.8 1.3 fusion.206
  26.5 0.8 fusion.97
  28.9 1.0 constant_dynamic-update-slice_fusion.2
  30.0 1.0 constant_dynamic-update-slice_fusion
  34.6 0.8 fusion.195
  35.6 0.9 fusion.196
  37.2 1.1 pad_maximum_fusion
  38.4 1.4 broadcast_multiply_fusion
  39.8 1.3 collective-permute-start.4
  41.1 3.7 %collective-permute-start.5 = (f32[4,1,128,128]{3,2,1,0:T(8,128)S(1)}, f32[4,1,128,128]{3,2,1,0:T(8,128)S(1)}, u32[]{:S(2)}, u32[]{:S(2)}) collective-permute-start(f32[4,1,128,128]{3,2,1,0:T(8,128)S(1)} %get-tuple-element.81), channel_id=1, source_target_pairs={{0,4},{4,8},{8,12},{1,5},{5,9},{9,13},{2,6},{6,10},{10,14},{3,7},{... | collective-permute-start | bytes 786440 | tf_op jit(solution)/shard_map/ppermute | solution.py:15
  45.1 0.8 collective-permute-done.5
  48.1 1.3 collective-permute-start.6
  49.5 6.4 %collective-permute-start.7 = (f32[4,1,128,128]{3,2,1,0:T(8,128)S(1)}, f32[4,1,128,128]{3,2,1,0:T(8,128)S(1)}, u32[]{:S(2)}, u32[]{:S(2)}) collective-permute-start(f32[4,1,128,128]{3,2,1,0:T(8,128)S(1)} %get-tuple-element.79), channel_id=1, source_target_pairs={{0,4},{4,8},{8,12},{1,5},{5,9},{9,13},{2,6},{6,10},{10,14},{3,7},{... | collective-permute-start | bytes 786440 | tf_op jit(solution)/shard_map/ppermute | solution.py:15
  56.2 0.9 collective-permute-done.7
  59.1 6.6 %collective-permute-start.9 = (f32[4,1,128,128]{3,2,1,0:T(8,128)S(1)}, f32[4,1,128,128]{3,2,1,0:T(8,128)S(1)}, u32[]{:S(2)}, u32[]{:S(2)}) collective-permute-start(f32[4,1,128,128]{3,2,1,0:T(8,128)S(1)} %get-tuple-element.77), channel_id=1, source_target_pairs={{0,4},{4,8},{8,12},{1,5},{5,9},{9,13},{2,6},{6,10},{10,14},{3,7},{... | collective-permute-start | bytes 786440 | tf_op jit(solution)/shard_map/ppermute | solution.py:15
  65.8 1.3 collective-permute-start.8
  67.3 3.9 %collective-permute-done.8 = f32[4,1,128,128]{3,2,1,0:T(8,128)S(1)} collective-permute-done((f32[4,1,128,128]{3,2,1,0:T(8,128)S(1)}, f32[4,1,128,128]{3,2,1,0:T(8,128)S(1)}, u32[]{:S(2)}, u32[]{:S(2)}) %collective-permute-start.8) | collective-permute-done | bytes 262176 | tf_op jit(solution)/shard_map/ppermute | solution.py:17
  73.2 6.7 %collective-permute-start.11 = (f32[4,1,128,128]{3,2,1,0:T(8,128)S(1)}, f32[4,1,128,128]{3,2,1,0:T(8,128)S(1)}, u32[]{:S(2)}, u32[]{:S(2)}) collective-permute-start(f32[4,1,128,128]{3,2,1,0:T(8,128)S(1)} %get-tuple-element.75), channel_id=1, source_target_pairs={{0,4},{4,8},{8,12},{1,5},{5,9},{9,13},{2,6},{6,10},{10,14},{3,7},{... | collective-permute-start | bytes 786440 | tf_op jit(solution)/shard_map/ppermute | solution.py:15
  80.1 1.3 collective-permute-start.10
  81.6 1.9 collective-permute-done.10
  85.6 6.4 %collective-permute-start.13 = (f32[4,1,128,128]{3,2,1,0:T(8,128)S(1)}, f32[4,1,128,128]{3,2,1,0:T(8,128)S(1)}, u32[]{:S(2)}, u32[]{:S(2)}) collective-permute-start(f32[4,1,128,128]{3,2,1,0:T(8,128)S(1)} %get-tuple-element.73), channel_id=1, source_target_pairs={{0,4},{4,8},{8,12},{1,5},{5,9},{9,13},{2,6},{6,10},{10,14},{3,7},{... | collective-permute-start | bytes 786440 | tf_op jit(solution)/shard_map/ppermute | solution.py:15
  92.1 1.3 collective-permute-start.12
  93.6 1.9 collective-permute-done.12
  97.5 6.2 %collective-permute-start.15 = (f32[4,1,128,128]{3,2,1,0:T(8,128)S(1)}, f32[4,1,128,128]{3,2,1,0:T(8,128)S(1)}, u32[]{:S(2)}, u32[]{:S(2)}) collective-permute-start(f32[4,1,128,128]{3,2,1,0:T(8,128)S(1)} %get-tuple-element.71), channel_id=1, source_target_pairs={{0,4},{4,8},{8,12},{1,5},{5,9},{9,13},{2,6},{6,10},{10,14},{3,7},{... | collective-permute-start | bytes 786440 | tf_op jit(solution)/shard_map/ppermute | solution.py:15
  103.8 1.3 collective-permute-start.14
  105.3 1.9 collective-permute-done.14
  109.2 6.2 %collective-permute-start.17 = (f32[4,1,128,128]{3,2,1,0:T(8,128)S(1)}, f32[4,1,128,128]{3,2,1,0:T(8,128)S(1)}, u32[]{:S(2)}, u32[]{:S(2)}) collective-permute-start(f32[4,1,128,128]{3,2,1,0:T(8,128)S(1)} %get-tuple-element.69), channel_id=1, source_target_pairs={{0,4},{4,8},{8,12},{1,5},{5,9},{9,13},{2,6},{6,10},{10,14},{3,7},{... | collective-permute-start | bytes 786440 | tf_op jit(solution)/shard_map/ppermute | solution.py:15
  115.7 1.3 collective-permute-start.16
  117.2 1.9 collective-permute-done.16
  121.1 3.7 %collective-permute-start.18 = (f32[4,2,128,128]{3,2,1,0:T(8,128)S(1)}, f32[4,2,128,128]{3,2,1,0:T(8,128)S(1)}, u32[]{:S(2)}, u32[]{:S(2)}) collective-permute-start(f32[4,2,128,128]{3,2,1,0:T(8,128)S(1)} %pad_maximum_fusion.2), channel_id=1, source_target_pairs={{0,3},{1,0},{2,1},{3,2},{4,7},{5,4},{6,5},{7,6},{8,11},{9,8},{10,9... | collective-permute-start | bytes 1572872 | tf_op jit(solution)/shard_map/ppermute | solution.py:27
  124.8 9.0 %collective-permute-done.18 = f32[4,2,128,128]{3,2,1,0:T(8,128)S(1)} collective-permute-done((f32[4,2,128,128]{3,2,1,0:T(8,128)S(1)}, f32[4,2,128,128]{3,2,1,0:T(8,128)S(1)}, u32[]{:S(2)}, u32[]{:S(2)}) %collective-permute-start.18) | collective-permute-done | bytes 524320 | tf_op jit(solution)/shard_map/ppermute | solution.py:27
  133.8 5.3 %collective-permute-start.20 = (f32[4,1,128,128]{3,2,1,0:T(8,128)S(1)}, f32[4,1,128,128]{3,2,1,0:T(8,128)S(1)}, u32[]{:S(2)}, u32[]{:S(2)}) collective-permute-start(f32[4,1,128,128]{3,2,1,0:T(8,128)S(1)} %get-tuple-element.51), channel_id=1, source_target_pairs={{0,4},{4,8},{8,12},{1,5},{5,9},{9,13},{2,6},{6,10},{10,14},{3,7},{... | collective-permute-start | bytes 786440 | tf_op jit(solution)/shard_map/ppermute | solution.py:15
  139.2 1.3 collective-permute-start.19
  140.5 2.1 collective-permute-done.19
  144.1 6.2 %collective-permute-start.22 = (f32[4,1,128,128]{3,2,1,0:T(8,128)S(1)}, f32[4,1,128,128]{3,2,1,0:T(8,128)S(1)}, u32[]{:S(2)}, u32[]{:S(2)}) collective-permute-start(f32[4,1,128,128]{3,2,1,0:T(8,128)S(1)} %get-tuple-element.49), channel_id=1, source_target_pairs={{0,4},{4,8},{8,12},{1,5},{5,9},{9,13},{2,6},{6,10},{10,14},{3,7},{... | collective-permute-start | bytes 786440 | tf_op jit(solution)/shard_map/ppermute | solution.py:15
  150.3 1.3 collective-permute-start.21
  151.7 2.1 collective-permute-done.21
  155.3 6.2 %collective-permute-start.24 = (f32[4,1,128,128]{3,2,1,0:T(8,128)S(1)}, f32[4,1,128,128]{3,2,1,0:T(8,128)S(1)}, u32[]{:S(2)}, u32[]{:S(2)}) collective-permute-start(f32[4,1,128,128]{3,2,1,0:T(8,128)S(1)} %get-tuple-element.47), channel_id=1, source_target_pairs={{0,4},{4,8},{8,12},{1,5},{5,9},{9,13},{2,6},{6,10},{10,14},{3,7},{... | collective-permute-start | bytes 786440 | tf_op jit(solution)/shard_map/ppermute | solution.py:15
  161.5 1.3 collective-permute-start.23
  162.8 2.1 collective-permute-done.23
  166.4 6.2 %collective-permute-start.26 = (f32[4,1,128,128]{3,2,1,0:T(8,128)S(1)}, f32[4,1,128,128]{3,2,1,0:T(8,128)S(1)}, u32[]{:S(2)}, u32[]{:S(2)}) collective-permute-start(f32[4,1,128,128]{3,2,1,0:T(8,128)S(1)} %get-tuple-element.45), channel_id=1, source_target_pairs={{0,4},{4,8},{8,12},{1,5},{5,9},{9,13},{2,6},{6,10},{10,14},{3,7},{... | collective-permute-start | bytes 786440 | tf_op jit(solution)/shard_map/ppermute | solution.py:15
  172.6 1.5 collective-permute-start.25
  174.2 1.9 collective-permute-done.25
  177.6 6.2 %collective-permute-start.28 = (f32[4,1,128,128]{3,2,1,0:T(8,128)S(1)}, f32[4,1,128,128]{3,2,1,0:T(8,128)S(1)}, u32[]{:S(2)}, u32[]{:S(2)}) collective-permute-start(f32[4,1,128,128]{3,2,1,0:T(8,128)S(1)} %get-tuple-element.43), channel_id=1, source_target_pairs={{0,4},{4,8},{8,12},{1,5},{5,9},{9,13},{2,6},{6,10},{10,14},{3,7},{... | collective-permute-start | bytes 786440 | tf_op jit(solution)/shard_map/ppermute | solution.py:15
  183.8 1.3 collective-permute-start.27
  185.1 2.1 collective-permute-done.27
  188.7 6.2 %collective-permute-start.30 = (f32[4,1,128,128]{3,2,1,0:T(8,128)S(1)}, f32[4,1,128,128]{3,2,1,0:T(8,128)S(1)}, u32[]{:S(2)}, u32[]{:S(2)}) collective-permute-start(f32[4,1,128,128]{3,2,1,0:T(8,128)S(1)} %get-tuple-element.41), channel_id=1, source_target_pairs={{0,4},{4,8},{8,12},{1,5},{5,9},{9,13},{2,6},{6,10},{10,14},{3,7},{... | collective-permute-start | bytes 786440 | tf_op jit(solution)/shard_map/ppermute | solution.py:15
  194.9 1.3 collective-permute-start.29
  196.2 2.1 collective-permute-done.29
  199.8 6.2 %collective-permute-start.32 = (f32[4,1,128,128]{3,2,1,0:T(8,128)S(1)}, f32[4,1,128,128]{3,2,1,0:T(8,128)S(1)}, u32[]{:S(2)}, u32[]{:S(2)}) collective-permute-start(f32[4,1,128,128]{3,2,1,0:T(8,128)S(1)} %get-tuple-element.39), channel_id=1, source_target_pairs={{0,4},{4,8},{8,12},{1,5},{5,9},{9,13},{2,6},{6,10},{10,14},{3,7},{... | collective-permute-start | bytes 786440 | tf_op jit(solution)/shard_map/ppermute | solution.py:15
  206.0 1.3 collective-permute-start.31
  207.4 2.1 collective-permute-done.31
  210.9 0.9 fusion.10
  211.9 1.2 add_multiply_fusion
  213.1 6.2 %collective-permute-start.34 = (f32[4,1,128,128]{3,2,1,0:T(8,128)S(1)}, f32[4,1,128,128]{3,2,1,0:T(8,128)S(1)}, u32[]{:S(2)}, u32[]{:S(2)}) collective-permute-start(f32[4,1,128,128]{3,2,1,0:T(8,128)S(1)} %get-tuple-element.37), channel_id=1, source_target_pairs={{0,4},{4,8},{8,12},{1,5},{5,9},{9,13},{2,6},{6,10},{10,14},{3,7},{... | collective-permute-start | bytes 786440 | tf_op jit(solution)/shard_map/ppermute | solution.py:15
  219.3 1.3 collective-permute-start.33
  220.6 34.2 %all-reduce.22.cloned.1.call-done = f32[2,128,128]{2,1,0:T(8,128)} async-done(((f32[2,128,128]{2,1,0:T(8,128)}), f32[2,128,128]{2,1,0:T(8,128)}) %all-reduce.22.cloned.1.call-update) | async-done | bytes 131088 | tf_op jit(solution)/shard_map/psum | solution.py:162
  254.8 1.4 constant_dynamic-slice_fusion
  258.2 0.8 maximum_bitcast_fusion
  (339 shorter events, 39.4 us)
Async XLA Ops:
  7.2 13.7 %copy-start = (bf16[8,2,128,128]{3,2,1,0:T(8,128)(2,1)S(1)}, bf16[8,2,128,128]{3,2,1,0:T(8,128)(2,1)}, u32[]{:S(2)}) copy-start(bf16[8,2,128,128]{3,2,1,0:T(8,128)(2,1)} %param.6) | copy-start | bytes 1572868
  7.2 247.6 %all-reduce.22.cloned.1.call-start = ((), (), s32[]{:S(2)}) async-start(), calls=%async_computation | async-start | bytes 262144 | tf_op jit(solution)/shard_map/psum | solution.py:162
  8.0 14.2 %copy-start.5 = (bf16[8,3,2,128,128]{4,3,2,1,0:T(8,128)(2,1)S(1)}, bf16[8,3,2,128,128]{4,3,2,1,0:T(8,128)(2,1)}, u32[]{:S(2)}) copy-start(bf16[8,3,2,128,128]{4,3,2,1,0:T(8,128)(2,1)} %param.5) | copy-start | bytes 4718596
  8.0 27.7 %collective-permute-start = (f32[4,1,128,128]{3,2,1,0:T(8,128)}, f32[4,1,128,128]{3,2,1,0:T(8,128)}, u32[]{:S(2)}, u32[]{:S(2)}) collective-permute-start(f32[4,1,128,128]{3,2,1,0:T(8,128)} %broadcast.302), channel_id=1, source_target_pairs={{4,0},{8,4},{12,8},{5,1},{9,5},{13,9},{6,2},{10,6},{14,10},{7,3},{... | collective-permute-start | bytes 786440 | tf_op jit(solution)/shard_map/ppermute | solution.py:17
  9.4 25.2 %collective-permute-start.1 = (f32[4,1,128,128]{3,2,1,0:T(8,128)}, f32[4,1,128,128]{3,2,1,0:T(8,128)}, u32[]{:S(2)}, u32[]{:S(2)}) collective-permute-start(f32[4,1,128,128]{3,2,1,0:T(8,128)} %broadcast.302), channel_id=1, source_target_pairs={{0,4},{4,8},{8,12},{1,5},{5,9},{9,13},{2,6},{6,10},{10,14},{3,7},{... | collective-permute-start | bytes 786440 | tf_op jit(solution)/shard_map/ppermute | solution.py:15
  15.0 13.9 %collective-permute-start.2 = (bf16[8,1,128,128]{3,2,1,0:T(8,128)(2,1)}, bf16[8,1,128,128]{3,2,1,0:T(8,128)(2,1)}, u32[]{:S(2)}, u32[]{:S(2)}) collective-permute-start(bf16[8,1,128,128]{3,2,1,0:T(8,128)(2,1)} %get-tuple-element.84), channel_id=1, source_target_pairs={{0,4},{4,8},{8,12},{1,5},{5,9},{9,13},{2,6},{6,10},{10,14},{3,7},{... | collective-permute-start | bytes 786440 | tf_op jit(solution)/shard_map/ppermute | solution.py:15
  19.5 10.5 %collective-permute-start.3 = (bf16[8,1,128,128]{3,2,1,0:T(8,128)(2,1)}, bf16[8,1,128,128]{3,2,1,0:T(8,128)(2,1)}, u32[]{:S(2)}, u32[]{:S(2)}) collective-permute-start(bf16[8,1,128,128]{3,2,1,0:T(8,128)(2,1)} %get-tuple-element.83), channel_id=1, source_target_pairs={{4,0},{8,4},{12,8},{5,1},{9,5},{13,9},{6,2},{10,6},{14,10},{7,3},{... | collective-permute-start | bytes 786440 | tf_op jit(solution)/shard_map/ppermute | solution.py:17
  22.2 10.2 %copy-start.7 = (f32[2,128,128]{2,1,0:T(8,128)}, f32[2,128,128]{2,1,0:T(8,128)S(1)}, u32[]{:S(2)}) copy-start(f32[2,128,128]{2,1,0:T(8,128)S(1)} %get-tuple-element.55) | copy-start | bytes 393220
  22.5 3.9 %copy-start.1 = (f32[1,3,2,128,128]{4,3,2,1,0:T(8,128)}, f32[1,3,2,128,128]{4,3,2,1,0:T(8,128)S(1)}, u32[]{:S(2)}) copy-start(f32[1,3,2,128,128]{4,3,2,1,0:T(8,128)S(1)} %get-tuple-element.26) | copy-start | bytes 1179652
  22.5 4.0 %copy-start.3 = (f32[1,3,2,128,128]{4,3,2,1,0:T(8,128)}, f32[1,3,2,128,128]{4,3,2,1,0:T(8,128)S(1)}, u32[]{:S(2)}) copy-start(f32[1,3,2,128,128]{4,3,2,1,0:T(8,128)S(1)} %get-tuple-element.27) | copy-start | bytes 1179652
  23.3 3.1 %copy-start.47 = (s32[2,128,128]{2,1,0:T(8,128)S(1)}, s32[2,128,128]{2,1,0:T(8,128)}, u32[]{:S(2)}) copy-start(s32[2,128,128]{2,1,0:T(8,128)} %param.8) | copy-start | bytes 393220
  23.3 3.1 %copy-start.57 = (f32[2,128,128]{2,1,0:T(8,128)S(1)}, f32[2,128,128]{2,1,0:T(8,128)}, u32[]{:S(2)}) copy-start(f32[2,128,128]{2,1,0:T(8,128)} %param.7) | copy-start | bytes 393220
  32.4 1.0 copy-start.11
  35.6 1.4 copy-start.4
  36.9 1.4 copy-start.17
  36.9 1.4 copy-start.18
  36.9 1.4 copy-start.19
  37.0 1.4 copy-start.46
  39.8 6.2 %copy-start.58 = (s32[128,128]{1,0:T(8,128)S(1)}, s32[128,128]{1,0:T(8,128)}, u32[]{:S(2)}) copy-start(s32[128,128]{1,0:T(8,128)} %param.9) | copy-start | bytes 196612
  39.8 5.3 %collective-permute-start.4 = (f32[4,1,128,128]{3,2,1,0:T(8,128)S(1)}, f32[4,1,128,128]{3,2,1,0:T(8,128)S(1)}, u32[]{:S(2)}, u32[]{:S(2)}) collective-permute-start(f32[4,1,128,128]{3,2,1,0:T(8,128)S(1)} %get-tuple-element.82), channel_id=1, source_target_pairs={{4,0},{8,4},{12,8},{5,1},{9,5},{13,9},{6,2},{10,6},{14,10},{7,3},{... | collective-permute-start | bytes 786440 | tf_op jit(solution)/shard_map/ppermute | solution.py:17
  41.1 4.8 %collective-permute-start.5 = (f32[4,1,128,128]{3,2,1,0:T(8,128)S(1)}, f32[4,1,128,128]{3,2,1,0:T(8,128)S(1)}, u32[]{:S(2)}, u32[]{:S(2)}) collective-permute-start(f32[4,1,128,128]{3,2,1,0:T(8,128)S(1)} %get-tuple-element.81), channel_id=1, source_target_pairs={{0,4},{4,8},{8,12},{1,5},{5,9},{9,13},{2,6},{6,10},{10,14},{3,7},{... | collective-permute-start | bytes 786440 | tf_op jit(solution)/shard_map/ppermute | solution.py:15
  44.9 1.3 copy-start.2
  46.5 1.1 copy-start.45
  48.1 8.0 %collective-permute-start.6 = (f32[4,1,128,128]{3,2,1,0:T(8,128)S(1)}, f32[4,1,128,128]{3,2,1,0:T(8,128)S(1)}, u32[]{:S(2)}, u32[]{:S(2)}) collective-permute-start(f32[4,1,128,128]{3,2,1,0:T(8,128)S(1)} %get-tuple-element.80), channel_id=1, source_target_pairs={{4,0},{8,4},{12,8},{5,1},{9,5},{13,9},{6,2},{10,6},{14,10},{7,3},{... | collective-permute-start | bytes 786440 | tf_op jit(solution)/shard_map/ppermute | solution.py:17
  49.5 7.6 %collective-permute-start.7 = (f32[4,1,128,128]{3,2,1,0:T(8,128)S(1)}, f32[4,1,128,128]{3,2,1,0:T(8,128)S(1)}, u32[]{:S(2)}, u32[]{:S(2)}) collective-permute-start(f32[4,1,128,128]{3,2,1,0:T(8,128)S(1)} %get-tuple-element.79), channel_id=1, source_target_pairs={{0,4},{4,8},{8,12},{1,5},{5,9},{9,13},{2,6},{6,10},{10,14},{3,7},{... | collective-permute-start | bytes 786440 | tf_op jit(solution)/shard_map/ppermute | solution.py:15
  57.5 1.0 copy-start.35
  58.5 7.1 %copy-start.9 = (f32[2,128,128]{2,1,0:T(8,128)S(1)}, f32[2,128,128]{2,1,0:T(8,128)}, u32[]{:S(2)}) copy-start(f32[2,128,128]{2,1,0:T(8,128)} %get-tuple-element.56) | copy-start | bytes 393220
  59.1 8.1 %collective-permute-start.9 = (f32[4,1,128,128]{3,2,1,0:T(8,128)S(1)}, f32[4,1,128,128]{3,2,1,0:T(8,128)S(1)}, u32[]{:S(2)}, u32[]{:S(2)}) collective-permute-start(f32[4,1,128,128]{3,2,1,0:T(8,128)S(1)} %get-tuple-element.77), channel_id=1, source_target_pairs={{0,4},{4,8},{8,12},{1,5},{5,9},{9,13},{2,6},{6,10},{10,14},{3,7},{... | collective-permute-start | bytes 786440 | tf_op jit(solution)/shard_map/ppermute | solution.py:15
  65.8 5.4 %collective-permute-start.8 = (f32[4,1,128,128]{3,2,1,0:T(8,128)S(1)}, f32[4,1,128,128]{3,2,1,0:T(8,128)S(1)}, u32[]{:S(2)}, u32[]{:S(2)}) collective-permute-start(f32[4,1,128,128]{3,2,1,0:T(8,128)S(1)} %get-tuple-element.78), channel_id=1, source_target_pairs={{4,0},{8,4},{12,8},{5,1},{9,5},{13,9},{6,2},{10,6},{14,10},{7,3},{... | collective-permute-start | bytes 786440 | tf_op jit(solution)/shard_map/ppermute | solution.py:17
  71.6 1.0 copy-start.32
  73.2 8.4 %collective-permute-start.11 = (f32[4,1,128,128]{3,2,1,0:T(8,128)S(1)}, f32[4,1,128,128]{3,2,1,0:T(8,128)S(1)}, u32[]{:S(2)}, u32[]{:S(2)}) collective-permute-start(f32[4,1,128,128]{3,2,1,0:T(8,128)S(1)} %get-tuple-element.75), channel_id=1, source_target_pairs={{0,4},{4,8},{8,12},{1,5},{5,9},{9,13},{2,6},{6,10},{10,14},{3,7},{... | collective-permute-start | bytes 786440 | tf_op jit(solution)/shard_map/ppermute | solution.py:15
  80.1 3.4 %collective-permute-start.10 = (f32[4,1,128,128]{3,2,1,0:T(8,128)S(1)}, f32[4,1,128,128]{3,2,1,0:T(8,128)S(1)}, u32[]{:S(2)}, u32[]{:S(2)}) collective-permute-start(f32[4,1,128,128]{3,2,1,0:T(8,128)S(1)} %get-tuple-element.76), channel_id=1, source_target_pairs={{4,0},{8,4},{12,8},{5,1},{9,5},{13,9},{6,2},{10,6},{14,10},{7,3},{... | collective-permute-start | bytes 786440 | tf_op jit(solution)/shard_map/ppermute | solution.py:17
  84.0 1.0 copy-start.29
  85.0 7.0 %copy-start.8 = (f32[2,128,128]{2,1,0:T(8,128)S(1)}, f32[2,128,128]{2,1,0:T(8,128)}, u32[]{:S(2)}) copy-start(f32[2,128,128]{2,1,0:T(8,128)} %copy-done.7) | copy-start | bytes 393220
  85.6 8.0 %collective-permute-start.13 = (f32[4,1,128,128]{3,2,1,0:T(8,128)S(1)}, f32[4,1,128,128]{3,2,1,0:T(8,128)S(1)}, u32[]{:S(2)}, u32[]{:S(2)}) collective-permute-start(f32[4,1,128,128]{3,2,1,0:T(8,128)S(1)} %get-tuple-element.73), channel_id=1, source_target_pairs={{0,4},{4,8},{8,12},{1,5},{5,9},{9,13},{2,6},{6,10},{10,14},{3,7},{... | collective-permute-start | bytes 786440 | tf_op jit(solution)/shard_map/ppermute | solution.py:15
  92.1 3.4 %collective-permute-start.12 = (f32[4,1,128,128]{3,2,1,0:T(8,128)S(1)}, f32[4,1,128,128]{3,2,1,0:T(8,128)S(1)}, u32[]{:S(2)}, u32[]{:S(2)}) collective-permute-start(f32[4,1,128,128]{3,2,1,0:T(8,128)S(1)} %get-tuple-element.74), channel_id=1, source_target_pairs={{4,0},{8,4},{12,8},{5,1},{9,5},{13,9},{6,2},{10,6},{14,10},{7,3},{... | collective-permute-start | bytes 786440 | tf_op jit(solution)/shard_map/ppermute | solution.py:17
  95.9 1.0 copy-start.26
  97.5 7.7 %collective-permute-start.15 = (f32[4,1,128,128]{3,2,1,0:T(8,128)S(1)}, f32[4,1,128,128]{3,2,1,0:T(8,128)S(1)}, u32[]{:S(2)}, u32[]{:S(2)}) collective-permute-start(f32[4,1,128,128]{3,2,1,0:T(8,128)S(1)} %get-tuple-element.71), channel_id=1, source_target_pairs={{0,4},{4,8},{8,12},{1,5},{5,9},{9,13},{2,6},{6,10},{10,14},{3,7},{... | collective-permute-start | bytes 786440 | tf_op jit(solution)/shard_map/ppermute | solution.py:15
  103.8 3.4 %collective-permute-start.14 = (f32[4,1,128,128]{3,2,1,0:T(8,128)S(1)}, f32[4,1,128,128]{3,2,1,0:T(8,128)S(1)}, u32[]{:S(2)}, u32[]{:S(2)}) collective-permute-start(f32[4,1,128,128]{3,2,1,0:T(8,128)S(1)} %get-tuple-element.72), channel_id=1, source_target_pairs={{4,0},{8,4},{12,8},{5,1},{9,5},{13,9},{6,2},{10,6},{14,10},{7,3},{... | collective-permute-start | bytes 786440 | tf_op jit(solution)/shard_map/ppermute | solution.py:17
  109.2 7.9 %collective-permute-start.17 = (f32[4,1,128,128]{3,2,1,0:T(8,128)S(1)}, f32[4,1,128,128]{3,2,1,0:T(8,128)S(1)}, u32[]{:S(2)}, u32[]{:S(2)}) collective-permute-start(f32[4,1,128,128]{3,2,1,0:T(8,128)S(1)} %get-tuple-element.69), channel_id=1, source_target_pairs={{0,4},{4,8},{8,12},{1,5},{5,9},{9,13},{2,6},{6,10},{10,14},{3,7},{... | collective-permute-start | bytes 786440 | tf_op jit(solution)/shard_map/ppermute | solution.py:15
  115.6 4.4 %copy-start.39 = (f32[1,2,128,128]{3,2,1,0:T(8,128)}, f32[1,2,128,128]{3,2,1,0:T(8,128)S(1)}, u32[]{:S(2)}) copy-start(f32[1,2,128,128]{3,2,1,0:T(8,128)S(1)} %get-tuple-element.189) | copy-start | bytes 393220
  115.6 4.4 %copy-start.41 = (f32[1,2,128,128]{3,2,1,0:T(8,128)}, f32[1,2,128,128]{3,2,1,0:T(8,128)S(1)}, u32[]{:S(2)}) copy-start(f32[1,2,128,128]{3,2,1,0:T(8,128)S(1)} %get-tuple-element.190) | copy-start | bytes 393220
  115.7 3.4 %collective-permute-start.16 = (f32[4,1,128,128]{3,2,1,0:T(8,128)S(1)}, f32[4,1,128,128]{3,2,1,0:T(8,128)S(1)}, u32[]{:S(2)}, u32[]{:S(2)}) collective-permute-start(f32[4,1,128,128]{3,2,1,0:T(8,128)S(1)} %get-tuple-element.70), channel_id=1, source_target_pairs={{4,0},{8,4},{12,8},{5,1},{9,5},{13,9},{6,2},{10,6},{14,10},{7,3},{... | collective-permute-start | bytes 786440 | tf_op jit(solution)/shard_map/ppermute | solution.py:17
  117.1 2.9 %copy-start.43 = (f32[1,2,128,128]{3,2,1,0:T(8,128)}, f32[1,2,128,128]{3,2,1,0:T(8,128)S(1)}, u32[]{:S(2)}) copy-start(f32[1,2,128,128]{3,2,1,0:T(8,128)S(1)} %fusion.27) | copy-start | bytes 393220
  119.5 1.0 copy-start.22
  121.1 12.7 %collective-permute-start.18 = (f32[4,2,128,128]{3,2,1,0:T(8,128)S(1)}, f32[4,2,128,128]{3,2,1,0:T(8,128)S(1)}, u32[]{:S(2)}, u32[]{:S(2)}) collective-permute-start(f32[4,2,128,128]{3,2,1,0:T(8,128)S(1)} %pad_maximum_fusion.2), channel_id=1, source_target_pairs={{0,3},{1,0},{2,1},{3,2},{4,7},{5,4},{6,5},{7,6},{8,11},{9,8},{10,9... | collective-permute-start | bytes 1572872 | tf_op jit(solution)/shard_map/ppermute | solution.py:27
  133.8 6.7 %collective-permute-start.20 = (f32[4,1,128,128]{3,2,1,0:T(8,128)S(1)}, f32[4,1,128,128]{3,2,1,0:T(8,128)S(1)}, u32[]{:S(2)}, u32[]{:S(2)}) collective-permute-start(f32[4,1,128,128]{3,2,1,0:T(8,128)S(1)} %get-tuple-element.51), channel_id=1, source_target_pairs={{0,4},{4,8},{8,12},{1,5},{5,9},{9,13},{2,6},{6,10},{10,14},{3,7},{... | collective-permute-start | bytes 786440 | tf_op jit(solution)/shard_map/ppermute | solution.py:15
  139.2 3.4 %collective-permute-start.19 = (f32[4,1,128,128]{3,2,1,0:T(8,128)S(1)}, f32[4,1,128,128]{3,2,1,0:T(8,128)S(1)}, u32[]{:S(2)}, u32[]{:S(2)}) collective-permute-start(f32[4,1,128,128]{3,2,1,0:T(8,128)S(1)} %get-tuple-element.52), channel_id=1, source_target_pairs={{4,0},{8,4},{12,8},{5,1},{9,5},{13,9},{6,2},{10,6},{14,10},{7,3},{... | collective-permute-start | bytes 786440 | tf_op jit(solution)/shard_map/ppermute | solution.py:17
  144.1 7.5 %collective-permute-start.22 = (f32[4,1,128,128]{3,2,1,0:T(8,128)S(1)}, f32[4,1,128,128]{3,2,1,0:T(8,128)S(1)}, u32[]{:S(2)}, u32[]{:S(2)}) collective-permute-start(f32[4,1,128,128]{3,2,1,0:T(8,128)S(1)} %get-tuple-element.49), channel_id=1, source_target_pairs={{0,4},{4,8},{8,12},{1,5},{5,9},{9,13},{2,6},{6,10},{10,14},{3,7},{... | collective-permute-start | bytes 786440 | tf_op jit(solution)/shard_map/ppermute | solution.py:15
  150.3 3.4 %collective-permute-start.21 = (f32[4,1,128,128]{3,2,1,0:T(8,128)S(1)}, f32[4,1,128,128]{3,2,1,0:T(8,128)S(1)}, u32[]{:S(2)}, u32[]{:S(2)}) collective-permute-start(f32[4,1,128,128]{3,2,1,0:T(8,128)S(1)} %get-tuple-element.50), channel_id=1, source_target_pairs={{4,0},{8,4},{12,8},{5,1},{9,5},{13,9},{6,2},{10,6},{14,10},{7,3},{... | collective-permute-start | bytes 786440 | tf_op jit(solution)/shard_map/ppermute | solution.py:17
  155.3 7.5 %collective-permute-start.24 = (f32[4,1,128,128]{3,2,1,0:T(8,128)S(1)}, f32[4,1,128,128]{3,2,1,0:T(8,128)S(1)}, u32[]{:S(2)}, u32[]{:S(2)}) collective-permute-start(f32[4,1,128,128]{3,2,1,0:T(8,128)S(1)} %get-tuple-element.47), channel_id=1, source_target_pairs={{0,4},{4,8},{8,12},{1,5},{5,9},{9,13},{2,6},{6,10},{10,14},{3,7},{... | collective-permute-start | bytes 786440 | tf_op jit(solution)/shard_map/ppermute | solution.py:15
  161.5 3.4 %collective-permute-start.23 = (f32[4,1,128,128]{3,2,1,0:T(8,128)S(1)}, f32[4,1,128,128]{3,2,1,0:T(8,128)S(1)}, u32[]{:S(2)}, u32[]{:S(2)}) collective-permute-start(f32[4,1,128,128]{3,2,1,0:T(8,128)S(1)} %get-tuple-element.48), channel_id=1, source_target_pairs={{4,0},{8,4},{12,8},{5,1},{9,5},{13,9},{6,2},{10,6},{14,10},{7,3},{... | collective-permute-start | bytes 786440 | tf_op jit(solution)/shard_map/ppermute | solution.py:17
  166.4 7.7 %collective-permute-start.26 = (f32[4,1,128,128]{3,2,1,0:T(8,128)S(1)}, f32[4,1,128,128]{3,2,1,0:T(8,128)S(1)}, u32[]{:S(2)}, u32[]{:S(2)}) collective-permute-start(f32[4,1,128,128]{3,2,1,0:T(8,128)S(1)} %get-tuple-element.45), channel_id=1, source_target_pairs={{0,4},{4,8},{8,12},{1,5},{5,9},{9,13},{2,6},{6,10},{10,14},{3,7},{... | collective-permute-start | bytes 786440 | tf_op jit(solution)/shard_map/ppermute | solution.py:15
  172.6 3.4 %collective-permute-start.25 = (f32[4,1,128,128]{3,2,1,0:T(8,128)S(1)}, f32[4,1,128,128]{3,2,1,0:T(8,128)S(1)}, u32[]{:S(2)}, u32[]{:S(2)}) collective-permute-start(f32[4,1,128,128]{3,2,1,0:T(8,128)S(1)} %get-tuple-element.46), channel_id=1, source_target_pairs={{4,0},{8,4},{12,8},{5,1},{9,5},{13,9},{6,2},{10,6},{14,10},{7,3},{... | collective-permute-start | bytes 786440 | tf_op jit(solution)/shard_map/ppermute | solution.py:17
  177.6 7.5 %collective-permute-start.28 = (f32[4,1,128,128]{3,2,1,0:T(8,128)S(1)}, f32[4,1,128,128]{3,2,1,0:T(8,128)S(1)}, u32[]{:S(2)}, u32[]{:S(2)}) collective-permute-start(f32[4,1,128,128]{3,2,1,0:T(8,128)S(1)} %get-tuple-element.43), channel_id=1, source_target_pairs={{0,4},{4,8},{8,12},{1,5},{5,9},{9,13},{2,6},{6,10},{10,14},{3,7},{... | collective-permute-start | bytes 786440 | tf_op jit(solution)/shard_map/ppermute | solution.py:15
  183.8 3.4 %collective-permute-start.27 = (f32[4,1,128,128]{3,2,1,0:T(8,128)S(1)}, f32[4,1,128,128]{3,2,1,0:T(8,128)S(1)}, u32[]{:S(2)}, u32[]{:S(2)}) collective-permute-start(f32[4,1,128,128]{3,2,1,0:T(8,128)S(1)} %get-tuple-element.44), channel_id=1, source_target_pairs={{4,0},{8,4},{12,8},{5,1},{9,5},{13,9},{6,2},{10,6},{14,10},{7,3},{... | collective-permute-start | bytes 786440 | tf_op jit(solution)/shard_map/ppermute | solution.py:17
  188.7 7.5 %collective-permute-start.30 = (f32[4,1,128,128]{3,2,1,0:T(8,128)S(1)}, f32[4,1,128,128]{3,2,1,0:T(8,128)S(1)}, u32[]{:S(2)}, u32[]{:S(2)}) collective-permute-start(f32[4,1,128,128]{3,2,1,0:T(8,128)S(1)} %get-tuple-element.41), channel_id=1, source_target_pairs={{0,4},{4,8},{8,12},{1,5},{5,9},{9,13},{2,6},{6,10},{10,14},{3,7},{... | collective-permute-start | bytes 786440 | tf_op jit(solution)/shard_map/ppermute | solution.py:15
  194.9 3.4 %collective-permute-start.29 = (f32[4,1,128,128]{3,2,1,0:T(8,128)S(1)}, f32[4,1,128,128]{3,2,1,0:T(8,128)S(1)}, u32[]{:S(2)}, u32[]{:S(2)}) collective-permute-start(f32[4,1,128,128]{3,2,1,0:T(8,128)S(1)} %get-tuple-element.42), channel_id=1, source_target_pairs={{4,0},{8,4},{12,8},{5,1},{9,5},{13,9},{6,2},{10,6},{14,10},{7,3},{... | collective-permute-start | bytes 786440 | tf_op jit(solution)/shard_map/ppermute | solution.py:17
  199.8 7.5 %collective-permute-start.32 = (f32[4,1,128,128]{3,2,1,0:T(8,128)S(1)}, f32[4,1,128,128]{3,2,1,0:T(8,128)S(1)}, u32[]{:S(2)}, u32[]{:S(2)}) collective-permute-start(f32[4,1,128,128]{3,2,1,0:T(8,128)S(1)} %get-tuple-element.39), channel_id=1, source_target_pairs={{0,4},{4,8},{8,12},{1,5},{5,9},{9,13},{2,6},{6,10},{10,14},{3,7},{... | collective-permute-start | bytes 786440 | tf_op jit(solution)/shard_map/ppermute | solution.py:15
  206.0 3.4 %collective-permute-start.31 = (f32[4,1,128,128]{3,2,1,0:T(8,128)S(1)}, f32[4,1,128,128]{3,2,1,0:T(8,128)S(1)}, u32[]{:S(2)}, u32[]{:S(2)}) collective-permute-start(f32[4,1,128,128]{3,2,1,0:T(8,128)S(1)} %get-tuple-element.40), channel_id=1, source_target_pairs={{4,0},{8,4},{12,8},{5,1},{9,5},{13,9},{6,2},{10,6},{14,10},{7,3},{... | collective-permute-start | bytes 786440 | tf_op jit(solution)/shard_map/ppermute | solution.py:17
  209.5 1.4 copy-start.6
  213.1 43.1 %collective-permute-start.34 = (f32[4,1,128,128]{3,2,1,0:T(8,128)S(1)}, f32[4,1,128,128]{3,2,1,0:T(8,128)S(1)}, u32[]{:S(2)}, u32[]{:S(2)}) collective-permute-start(f32[4,1,128,128]{3,2,1,0:T(8,128)S(1)} %get-tuple-element.37), channel_id=1, source_target_pairs={{0,4},{4,8},{8,12},{1,5},{5,9},{9,13},{2,6},{6,10},{10,14},{3,7},{... | collective-permute-start | bytes 786440 | tf_op jit(solution)/shard_map/ppermute | solution.py:15
  219.3 36.9 %collective-permute-start.33 = (f32[4,1,128,128]{3,2,1,0:T(8,128)S(1)}, f32[4,1,128,128]{3,2,1,0:T(8,128)S(1)}, u32[]{:S(2)}, u32[]{:S(2)}) collective-permute-start(f32[4,1,128,128]{3,2,1,0:T(8,128)S(1)} %get-tuple-element.38), channel_id=1, source_target_pairs={{4,0},{8,4},{12,8},{5,1},{9,5},{13,9},{6,2},{10,6},{14,10},{7,3},{... | collective-permute-start | bytes 786440 | tf_op jit(solution)/shard_map/ppermute | solution.py:17
  256.6 1.1 copy-start.44
  (31 other events, 29.4 us)
Sparse Core Ops, SparseCore 0:
  219.4 35.3 all-reduce.21
where the time goes:
time: 267 us; the launch traced here: 266 us
  starting transfers between devices  125 us (47%)
  waiting for transfers between devices  71 us (27%)
  other arithmetic  37.5 us (14%)
  local copies, waits for them, and re-layouts  16.4 us (6%)
  between operations  16.1 us (6%)
    ppermute x17, starting transfers between devices, padded(): lax.ppermute(tail, axis, [(i, (i + 1) % count) for i in range(ends)])  99 us
    psum x1, waiting for transfers between devices, body(): summed = lax.psum(partial_sum, 'arc')  34.2 us
    ppermute x17, waiting for transfers between devices, padded(): lax.ppermute(head, axis, [((i + 1) % count, i) for i in range(ends)])  26 us
    ppermute x17, starting transfers between devices, padded(): lax.ppermute(head, axis, [((i + 1) % count, i) for i in range(ends)])  22.3 us
    ppermute x1, waiting for transfers between devices, passed_along(): return lax.ppermute(value, axis, pairs)  9.02 us
    concatenate x16, other arithmetic, padded(): jnp.concatenate([lax.ppermute(tail, axis, [(i, (i + 1) % count) for i in...  8.71 us
    unnamed x120, local copies, waits for them, and re-layouts  8.05 us
    add x14, other arithmetic, adjoint_update(): a_now + 0.1 * (1.2 * laplace(ext_a) + carry_a - alpha * a_now - current_a...  7.44 us
  transfers between devices with their start and end apart: 36, of which 16 were waited for; matrix products, arithmetic and copies ran while one was open for 7% of the time, Pallas kernels for 0%

commit v1 on v0

--- a/solution.py
+++ b/solution.py
@@ -159,7 +159,9 @@
     for interior_block in range(device_instant_total - 1, -1, -1):
         adj, summand_contribution = one_step(adj, interior_block)
         partial_sum = partial_sum + summand_contribution
-    summed = lax.psum(partial_sum, "arc")
+    summed = partial_sum
+    for hop in (1, 2):
+        summed = summed + lax.ppermute(summed, "arc", [(dev, dev ^ hop) for dev in range(4)])
     share = summed.shape[1] // lax.axis_size("arc")
     gradient = lax.dynamic_slice_in_dim(summed, lax.axis_index("arc") * share, share, 1)
     return (gradient, adj[None])

time: 267 us -> 228 us (0.85)
  waiting for transfers between devices: 71 us -> 43.9 us
  between operations: 16.1 us -> 2.68 us
  starting transfers between devices: 125 us -> 128 us
    psum x1 -> x0, waiting for transfers between devices: 34.2 us -> none  [body(): summed = lax.psum(partial_sum, 'arc')]
    ppermute x0 -> x2, waiting for transfers between devices: none -> 7.06 us  [body(): lax.ppermute(summed, 'arc', [(dev, dev ^ hop) for dev in range(4)])]
    ppermute x0 -> x2, starting transfers between devices: none -> 3.1 us  [body(): lax.ppermute(summed, 'arc', [(dev, dev ^ hop) for dev in range(4)])]
  transfers between devices with their start and end apart: 36 -> 37, of which waited for: 16 -> 17; matrix products, arithmetic and copies ran while one was open for 7% -> 8% of each run, Pallas kernels for 0% -> 0%
where the time goes in v1:
time: 228 us; the launch traced here: 227 us
  starting transfers between devices  128 us (56%)
  waiting for transfers between devices  43.9 us (19%)
  other arithmetic  37.4 us (16%)
  local copies, waits for them, and re-layouts  14.9 us (7%)
  between operations  2.68 us (1%)
    ppermute x17, starting transfers between devices, padded(): lax.ppermute(tail, axis, [(i, (i + 1) % count) for i in range(ends)])  98.8 us
    ppermute x17, waiting for transfers between devices, padded(): lax.ppermute(head, axis, [((i + 1) % count, i) for i in range(ends)])  26 us
    ppermute x17, starting transfers between devices, padded(): lax.ppermute(head, axis, [((i + 1) % count, i) for i in range(ends)])  22.5 us
    ppermute x1, waiting for transfers between devices, passed_along(): return lax.ppermute(value, axis, pairs)  9.02 us
    concatenate x16, other arithmetic, padded(): jnp.concatenate([lax.ppermute(tail, axis, [(i, (i + 1) % count) for i in...  8.72 us
    unnamed x120, local copies, waits for them, and re-layouts  7.9 us
    add x14, other arithmetic, adjoint_update(): a_now + 0.1 * (1.2 * laplace(ext_a) + carry_a - alpha * a_now - current_a...  7.44 us
    ppermute x2, waiting for transfers between devices, body(): lax.ppermute(summed, 'arc', [(dev, dev ^ hop) for dev in range(4)])  7.06 us
  transfers between devices with their start and end apart: 37, of which 17 were waited for; matrix products, arithmetic and copies ran while one was open for 8% of the time, Pallas kernels for 0%

profile of v1, /device:TPU:0, one launch (start us, length us, event | category | flops | bytes accessed | tf_op | source)
XLA Modules:
  0.0 226.8 jit_solution(4099403826834384544)
XLA Ops:
  1.4 1.4 collective-permute-start
  2.8 3.7 %collective-permute-start.1 = (f32[4,1,128,128]{3,2,1,0:T(8,128)}, f32[4,1,128,128]{3,2,1,0:T(8,128)}, u32[]{:S(2)}, u32[]{:S(2)}) collective-permute-start(f32[4,1,128,128]{3,2,1,0:T(8,128)} %broadcast.302), channel_id=1, source_target_pairs={{0,4},{4,8},{8,12},{1,5},{5,9},{9,13},{2,6},{6,10},{10,14},{3,7},{... | collective-permute-start | bytes 786440 | tf_op jit(solution)/shard_map/ppermute | solution.py:15
  6.5 1.9 fusion.209
  8.4 4.5 %collective-permute-start.2 = (bf16[8,1,128,128]{3,2,1,0:T(8,128)(2,1)}, bf16[8,1,128,128]{3,2,1,0:T(8,128)(2,1)}, u32[]{:S(2)}, u32[]{:S(2)}) collective-permute-start(bf16[8,1,128,128]{3,2,1,0:T(8,128)(2,1)} %get-tuple-element.84), channel_id=1, source_target_pairs={{0,4},{4,8},{8,12},{1,5},{5,9},{9,13},{2,6},{6,10},{10,14},{3,7},{... | collective-permute-start | bytes 786440 | tf_op jit(solution)/shard_map/ppermute | solution.py:15
  12.9 1.3 collective-permute-start.3
  14.2 1.3 fusion.206
  19.8 0.9 fusion.97
  22.2 1.0 constant_dynamic-update-slice_fusion.2
  23.3 1.0 constant_dynamic-update-slice_fusion
  27.9 0.8 fusion.195
  28.9 0.9 fusion.196
  30.5 1.1 pad_maximum_fusion
  31.7 1.4 broadcast_multiply_fusion
  33.1 1.3 collective-permute-start.4
  34.4 3.7 %collective-permute-start.5 = (f32[4,1,128,128]{3,2,1,0:T(8,128)S(1)}, f32[4,1,128,128]{3,2,1,0:T(8,128)S(1)}, u32[]{:S(2)}, u32[]{:S(2)}) collective-permute-start(f32[4,1,128,128]{3,2,1,0:T(8,128)S(1)} %get-tuple-element.81), channel_id=1, source_target_pairs={{0,4},{4,8},{8,12},{1,5},{5,9},{9,13},{2,6},{6,10},{10,14},{3,7},{... | collective-permute-start | bytes 786440 | tf_op jit(solution)/shard_map/ppermute | solution.py:15
  38.4 0.8 collective-permute-done.5
  41.4 1.3 collective-permute-start.6
  42.8 6.4 %collective-permute-start.7 = (f32[4,1,128,128]{3,2,1,0:T(8,128)S(1)}, f32[4,1,128,128]{3,2,1,0:T(8,128)S(1)}, u32[]{:S(2)}, u32[]{:S(2)}) collective-permute-start(f32[4,1,128,128]{3,2,1,0:T(8,128)S(1)} %get-tuple-element.79), channel_id=1, source_target_pairs={{0,4},{4,8},{8,12},{1,5},{5,9},{9,13},{2,6},{6,10},{10,14},{3,7},{... | collective-permute-start | bytes 786440 | tf_op jit(solution)/shard_map/ppermute | solution.py:15
  49.4 0.9 collective-permute-done.7
  52.4 6.6 %collective-permute-start.9 = (f32[4,1,128,128]{3,2,1,0:T(8,128)S(1)}, f32[4,1,128,128]{3,2,1,0:T(8,128)S(1)}, u32[]{:S(2)}, u32[]{:S(2)}) collective-permute-start(f32[4,1,128,128]{3,2,1,0:T(8,128)S(1)} %get-tuple-element.77), channel_id=1, source_target_pairs={{0,4},{4,8},{8,12},{1,5},{5,9},{9,13},{2,6},{6,10},{10,14},{3,7},{... | collective-permute-start | bytes 786440 | tf_op jit(solution)/shard_map/ppermute | solution.py:15
  59.0 1.3 collective-permute-start.8
  60.6 3.9 %collective-permute-done.8 = f32[4,1,128,128]{3,2,1,0:T(8,128)S(1)} collective-permute-done((f32[4,1,128,128]{3,2,1,0:T(8,128)S(1)}, f32[4,1,128,128]{3,2,1,0:T(8,128)S(1)}, u32[]{:S(2)}, u32[]{:S(2)}) %collective-permute-start.8) | collective-permute-done | bytes 262176 | tf_op jit(solution)/shard_map/ppermute | solution.py:17
  66.5 6.7 %collective-permute-start.11 = (f32[4,1,128,128]{3,2,1,0:T(8,128)S(1)}, f32[4,1,128,128]{3,2,1,0:T(8,128)S(1)}, u32[]{:S(2)}, u32[]{:S(2)}) collective-permute-start(f32[4,1,128,128]{3,2,1,0:T(8,128)S(1)} %get-tuple-element.75), channel_id=1, source_target_pairs={{0,4},{4,8},{8,12},{1,5},{5,9},{9,13},{2,6},{6,10},{10,14},{3,7},{... | collective-permute-start | bytes 786440 | tf_op jit(solution)/shard_map/ppermute | solution.py:15
  73.4 1.3 collective-permute-start.10
  74.9 1.9 collective-permute-done.10
  78.9 6.2 %collective-permute-start.13 = (f32[4,1,128,128]{3,2,1,0:T(8,128)S(1)}, f32[4,1,128,128]{3,2,1,0:T(8,128)S(1)}, u32[]{:S(2)}, u32[]{:S(2)}) collective-permute-start(f32[4,1,128,128]{3,2,1,0:T(8,128)S(1)} %get-tuple-element.73), channel_id=1, source_target_pairs={{0,4},{4,8},{8,12},{1,5},{5,9},{9,13},{2,6},{6,10},{10,14},{3,7},{... | collective-permute-start | bytes 786440 | tf_op jit(solution)/shard_map/ppermute | solution.py:15
  85.2 1.5 collective-permute-start.12
  86.9 1.9 collective-permute-done.12
  90.8 6.2 %collective-permute-start.15 = (f32[4,1,128,128]{3,2,1,0:T(8,128)S(1)}, f32[4,1,128,128]{3,2,1,0:T(8,128)S(1)}, u32[]{:S(2)}, u32[]{:S(2)}) collective-permute-start(f32[4,1,128,128]{3,2,1,0:T(8,128)S(1)} %get-tuple-element.71), channel_id=1, source_target_pairs={{0,4},{4,8},{8,12},{1,5},{5,9},{9,13},{2,6},{6,10},{10,14},{3,7},{... | collective-permute-start | bytes 786440 | tf_op jit(solution)/shard_map/ppermute | solution.py:15
  97.1 1.3 collective-permute-start.14
  98.6 1.9 collective-permute-done.14
  102.5 6.2 %collective-permute-start.17 = (f32[4,1,128,128]{3,2,1,0:T(8,128)S(1)}, f32[4,1,128,128]{3,2,1,0:T(8,128)S(1)}, u32[]{:S(2)}, u32[]{:S(2)}) collective-permute-start(f32[4,1,128,128]{3,2,1,0:T(8,128)S(1)} %get-tuple-element.69), channel_id=1, source_target_pairs={{0,4},{4,8},{8,12},{1,5},{5,9},{9,13},{2,6},{6,10},{10,14},{3,7},{... | collective-permute-start | bytes 786440 | tf_op jit(solution)/shard_map/ppermute | solution.py:15
  108.9 1.3 collective-permute-start.16
  110.5 1.9 collective-permute-done.16
  114.4 3.7 %collective-permute-start.18 = (f32[4,2,128,128]{3,2,1,0:T(8,128)S(1)}, f32[4,2,128,128]{3,2,1,0:T(8,128)S(1)}, u32[]{:S(2)}, u32[]{:S(2)}) collective-permute-start(f32[4,2,128,128]{3,2,1,0:T(8,128)S(1)} %pad_maximum_fusion.2), channel_id=1, source_target_pairs={{0,3},{1,0},{2,1},{3,2},{4,7},{5,4},{6,5},{7,6},{8,11},{9,8},{10,9... | collective-permute-start | bytes 1572872 | tf_op jit(solution)/shard_map/ppermute | solution.py:27
  118.1 9.0 %collective-permute-done.18 = f32[4,2,128,128]{3,2,1,0:T(8,128)S(1)} collective-permute-done((f32[4,2,128,128]{3,2,1,0:T(8,128)S(1)}, f32[4,2,128,128]{3,2,1,0:T(8,128)S(1)}, u32[]{:S(2)}, u32[]{:S(2)}) %collective-permute-start.18) | collective-permute-done | bytes 524320 | tf_op jit(solution)/shard_map/ppermute | solution.py:27
  127.1 5.3 %collective-permute-start.20 = (f32[4,1,128,128]{3,2,1,0:T(8,128)S(1)}, f32[4,1,128,128]{3,2,1,0:T(8,128)S(1)}, u32[]{:S(2)}, u32[]{:S(2)}) collective-permute-start(f32[4,1,128,128]{3,2,1,0:T(8,128)S(1)} %get-tuple-element.51), channel_id=1, source_target_pairs={{0,4},{4,8},{8,12},{1,5},{5,9},{9,13},{2,6},{6,10},{10,14},{3,7},{... | collective-permute-start | bytes 786440 | tf_op jit(solution)/shard_map/ppermute | solution.py:15
  132.5 1.3 collective-permute-start.19
  133.8 2.1 collective-permute-done.19
  137.4 6.2 %collective-permute-start.22 = (f32[4,1,128,128]{3,2,1,0:T(8,128)S(1)}, f32[4,1,128,128]{3,2,1,0:T(8,128)S(1)}, u32[]{:S(2)}, u32[]{:S(2)}) collective-permute-start(f32[4,1,128,128]{3,2,1,0:T(8,128)S(1)} %get-tuple-element.49), channel_id=1, source_target_pairs={{0,4},{4,8},{8,12},{1,5},{5,9},{9,13},{2,6},{6,10},{10,14},{3,7},{... | collective-permute-start | bytes 786440 | tf_op jit(solution)/shard_map/ppermute | solution.py:15
  143.6 1.3 collective-permute-start.21
  144.9 2.1 collective-permute-done.21
  148.6 6.2 %collective-permute-start.24 = (f32[4,1,128,128]{3,2,1,0:T(8,128)S(1)}, f32[4,1,128,128]{3,2,1,0:T(8,128)S(1)}, u32[]{:S(2)}, u32[]{:S(2)}) collective-permute-start(f32[4,1,128,128]{3,2,1,0:T(8,128)S(1)} %get-tuple-element.47), channel_id=1, source_target_pairs={{0,4},{4,8},{8,12},{1,5},{5,9},{9,13},{2,6},{6,10},{10,14},{3,7},{... | collective-permute-start | bytes 786440 | tf_op jit(solution)/shard_map/ppermute | solution.py:15
  154.8 1.3 collective-permute-start.23
  156.1 2.1 collective-permute-done.23
  159.7 6.2 %collective-permute-start.26 = (f32[4,1,128,128]{3,2,1,0:T(8,128)S(1)}, f32[4,1,128,128]{3,2,1,0:T(8,128)S(1)}, u32[]{:S(2)}, u32[]{:S(2)}) collective-permute-start(f32[4,1,128,128]{3,2,1,0:T(8,128)S(1)} %get-tuple-element.45), channel_id=1, source_target_pairs={{0,4},{4,8},{8,12},{1,5},{5,9},{9,13},{2,6},{6,10},{10,14},{3,7},{... | collective-permute-start | bytes 786440 | tf_op jit(solution)/shard_map/ppermute | solution.py:15
  165.9 1.5 collective-permute-start.25
  167.5 1.9 collective-permute-done.25
  170.9 6.2 %collective-permute-start.28 = (f32[4,1,128,128]{3,2,1,0:T(8,128)S(1)}, f32[4,1,128,128]{3,2,1,0:T(8,128)S(1)}, u32[]{:S(2)}, u32[]{:S(2)}) collective-permute-start(f32[4,1,128,128]{3,2,1,0:T(8,128)S(1)} %get-tuple-element.43), channel_id=1, source_target_pairs={{0,4},{4,8},{8,12},{1,5},{5,9},{9,13},{2,6},{6,10},{10,14},{3,7},{... | collective-permute-start | bytes 786440 | tf_op jit(solution)/shard_map/ppermute | solution.py:15
  177.0 1.3 collective-permute-start.27
  178.4 2.1 collective-permute-done.27
  182.0 6.2 %collective-permute-start.30 = (f32[4,1,128,128]{3,2,1,0:T(8,128)S(1)}, f32[4,1,128,128]{3,2,1,0:T(8,128)S(1)}, u32[]{:S(2)}, u32[]{:S(2)}) collective-permute-start(f32[4,1,128,128]{3,2,1,0:T(8,128)S(1)} %get-tuple-element.41), channel_id=1, source_target_pairs={{0,4},{4,8},{8,12},{1,5},{5,9},{9,13},{2,6},{6,10},{10,14},{3,7},{... | collective-permute-start | bytes 786440 | tf_op jit(solution)/shard_map/ppermute | solution.py:15
  188.2 1.3 collective-permute-start.29
  189.5 2.1 collective-permute-done.29
  193.1 6.2 %collective-permute-start.32 = (f32[4,1,128,128]{3,2,1,0:T(8,128)S(1)}, f32[4,1,128,128]{3,2,1,0:T(8,128)S(1)}, u32[]{:S(2)}, u32[]{:S(2)}) collective-permute-start(f32[4,1,128,128]{3,2,1,0:T(8,128)S(1)} %get-tuple-element.39), channel_id=1, source_target_pairs={{0,4},{4,8},{8,12},{1,5},{5,9},{9,13},{2,6},{6,10},{10,14},{3,7},{... | collective-permute-start | bytes 786440 | tf_op jit(solution)/shard_map/ppermute | solution.py:15
  199.3 1.3 collective-permute-start.31
  200.7 2.1 collective-permute-done.31
  204.2 0.9 fusion.10
  205.7 6.2 %collective-permute-start.36 = (f32[4,1,128,128]{3,2,1,0:T(8,128)S(1)}, f32[4,1,128,128]{3,2,1,0:T(8,128)S(1)}, u32[]{:S(2)}, u32[]{:S(2)}) collective-permute-start(f32[4,1,128,128]{3,2,1,0:T(8,128)S(1)} %get-tuple-element.37), channel_id=1, source_target_pairs={{0,4},{4,8},{8,12},{1,5},{5,9},{9,13},{2,6},{6,10},{10,14},{3,7},{... | collective-permute-start | bytes 786440 | tf_op jit(solution)/shard_map/ppermute | solution.py:15
  212.1 1.3 collective-permute-start.35
  213.4 3.9 %collective-permute-done.33 = f32[2,128,128]{2,1,0:T(8,128)S(1)} collective-permute-done((f32[2,128,128]{2,1,0:T(8,128)S(1)}, f32[2,128,128]{2,1,0:T(8,128)S(1)}, u32[]{:S(2)}, u32[]{:S(2)}) %collective-permute-start.33) | collective-permute-done | bytes 131104 | tf_op jit(solution)/shard_map/ppermute | solution.py:164
  217.4 2.9 %collective-permute-start.34 = (f32[2,128,128]{2,1,0:T(8,128)S(1)}, f32[2,128,128]{2,1,0:T(8,128)S(1)}, u32[]{:S(2)}, u32[]{:S(2)}) collective-permute-start(f32[2,128,128]{2,1,0:T(8,128)S(1)} %add.1312), channel_id=1, source_target_pairs={{0,2},{1,3},{2,0},{3,1},{4,6},{5,7},{6,4},{7,5},{8,10},{9,11},{10,... | collective-permute-start | bytes 393224 | tf_op jit(solution)/shard_map/ppermute | solution.py:164
  222.2 0.8 maximum_bitcast_fusion
  223.0 3.1 %collective-permute-done.34 = f32[2,128,128]{2,1,0:T(8,128)S(1)} collective-permute-done((f32[2,128,128]{2,1,0:T(8,128)S(1)}, f32[2,128,128]{2,1,0:T(8,128)S(1)}, u32[]{:S(2)}, u32[]{:S(2)}) %collective-permute-start.34) | collective-permute-done | bytes 131104 | tf_op jit(solution)/shard_map/ppermute | solution.py:164
  (341 shorter events, 40.5 us)
Async XLA Ops:
  0.6 13.6 %copy-start = (bf16[8,2,128,128]{3,2,1,0:T(8,128)(2,1)S(1)}, bf16[8,2,128,128]{3,2,1,0:T(8,128)(2,1)}, u32[]{:S(2)}) copy-start(bf16[8,2,128,128]{3,2,1,0:T(8,128)(2,1)} %param.6) | copy-start | bytes 1572868
  1.4 14.2 %copy-start.5 = (bf16[8,3,2,128,128]{4,3,2,1,0:T(8,128)(2,1)S(1)}, bf16[8,3,2,128,128]{4,3,2,1,0:T(8,128)(2,1)}, u32[]{:S(2)}) copy-start(bf16[8,3,2,128,128]{4,3,2,1,0:T(8,128)(2,1)} %param.5) | copy-start | bytes 4718596
  1.4 27.5 %collective-permute-start = (f32[4,1,128,128]{3,2,1,0:T(8,128)}, f32[4,1,128,128]{3,2,1,0:T(8,128)}, u32[]{:S(2)}, u32[]{:S(2)}) collective-permute-start(f32[4,1,128,128]{3,2,1,0:T(8,128)} %broadcast.302), channel_id=1, source_target_pairs={{4,0},{8,4},{12,8},{5,1},{9,5},{13,9},{6,2},{10,6},{14,10},{7,3},{... | collective-permute-start | bytes 786440 | tf_op jit(solution)/shard_map/ppermute | solution.py:17
  2.8 25.1 %collective-permute-start.1 = (f32[4,1,128,128]{3,2,1,0:T(8,128)}, f32[4,1,128,128]{3,2,1,0:T(8,128)}, u32[]{:S(2)}, u32[]{:S(2)}) collective-permute-start(f32[4,1,128,128]{3,2,1,0:T(8,128)} %broadcast.302), channel_id=1, source_target_pairs={{0,4},{4,8},{8,12},{1,5},{5,9},{9,13},{2,6},{6,10},{10,14},{3,7},{... | collective-permute-start | bytes 786440 | tf_op jit(solution)/shard_map/ppermute | solution.py:15
  8.4 13.8 %collective-permute-start.2 = (bf16[8,1,128,128]{3,2,1,0:T(8,128)(2,1)}, bf16[8,1,128,128]{3,2,1,0:T(8,128)(2,1)}, u32[]{:S(2)}, u32[]{:S(2)}) collective-permute-start(bf16[8,1,128,128]{3,2,1,0:T(8,128)(2,1)} %get-tuple-element.84), channel_id=1, source_target_pairs={{0,4},{4,8},{8,12},{1,5},{5,9},{9,13},{2,6},{6,10},{10,14},{3,7},{... | collective-permute-start | bytes 786440 | tf_op jit(solution)/shard_map/ppermute | solution.py:15
  12.9 10.4 %collective-permute-start.3 = (bf16[8,1,128,128]{3,2,1,0:T(8,128)(2,1)}, bf16[8,1,128,128]{3,2,1,0:T(8,128)(2,1)}, u32[]{:S(2)}, u32[]{:S(2)}) collective-permute-start(bf16[8,1,128,128]{3,2,1,0:T(8,128)(2,1)} %get-tuple-element.83), channel_id=1, source_target_pairs={{4,0},{8,4},{12,8},{5,1},{9,5},{13,9},{6,2},{10,6},{14,10},{7,3},{... | collective-permute-start | bytes 786440 | tf_op jit(solution)/shard_map/ppermute | solution.py:17
  15.5 10.1 %copy-start.7 = (f32[2,128,128]{2,1,0:T(8,128)}, f32[2,128,128]{2,1,0:T(8,128)S(1)}, u32[]{:S(2)}) copy-start(f32[2,128,128]{2,1,0:T(8,128)S(1)} %get-tuple-element.55) | copy-start | bytes 393220
  15.9 3.9 %copy-start.1 = (f32[1,3,2,128,128]{4,3,2,1,0:T(8,128)}, f32[1,3,2,128,128]{4,3,2,1,0:T(8,128)S(1)}, u32[]{:S(2)}) copy-start(f32[1,3,2,128,128]{4,3,2,1,0:T(8,128)S(1)} %get-tuple-element.26) | copy-start | bytes 1179652
  15.9 3.9 %copy-start.3 = (f32[1,3,2,128,128]{4,3,2,1,0:T(8,128)}, f32[1,3,2,128,128]{4,3,2,1,0:T(8,128)S(1)}, u32[]{:S(2)}) copy-start(f32[1,3,2,128,128]{4,3,2,1,0:T(8,128)S(1)} %get-tuple-element.27) | copy-start | bytes 1179652
  16.7 3.0 %copy-start.47 = (s32[2,128,128]{2,1,0:T(8,128)S(1)}, s32[2,128,128]{2,1,0:T(8,128)}, u32[]{:S(2)}) copy-start(s32[2,128,128]{2,1,0:T(8,128)} %param.8) | copy-start | bytes 393220
  16.7 3.0 %copy-start.57 = (f32[2,128,128]{2,1,0:T(8,128)S(1)}, f32[2,128,128]{2,1,0:T(8,128)}, u32[]{:S(2)}) copy-start(f32[2,128,128]{2,1,0:T(8,128)} %param.7) | copy-start | bytes 393220
  25.6 1.0 copy-start.11
  28.9 1.4 copy-start.4
  30.2 1.4 copy-start.17
  30.2 1.4 copy-start.18
  30.2 1.4 copy-start.19
  30.2 1.4 copy-start.46
  33.1 6.2 %copy-start.58 = (s32[128,128]{1,0:T(8,128)S(1)}, s32[128,128]{1,0:T(8,128)}, u32[]{:S(2)}) copy-start(s32[128,128]{1,0:T(8,128)} %param.9) | copy-start | bytes 196612
  33.1 5.3 %collective-permute-start.4 = (f32[4,1,128,128]{3,2,1,0:T(8,128)S(1)}, f32[4,1,128,128]{3,2,1,0:T(8,128)S(1)}, u32[]{:S(2)}, u32[]{:S(2)}) collective-permute-start(f32[4,1,128,128]{3,2,1,0:T(8,128)S(1)} %get-tuple-element.82), channel_id=1, source_target_pairs={{4,0},{8,4},{12,8},{5,1},{9,5},{13,9},{6,2},{10,6},{14,10},{7,3},{... | collective-permute-start | bytes 786440 | tf_op jit(solution)/shard_map/ppermute | solution.py:17
  34.4 4.8 %collective-permute-start.5 = (f32[4,1,128,128]{3,2,1,0:T(8,128)S(1)}, f32[4,1,128,128]{3,2,1,0:T(8,128)S(1)}, u32[]{:S(2)}, u32[]{:S(2)}) collective-permute-start(f32[4,1,128,128]{3,2,1,0:T(8,128)S(1)} %get-tuple-element.81), channel_id=1, source_target_pairs={{0,4},{4,8},{8,12},{1,5},{5,9},{9,13},{2,6},{6,10},{10,14},{3,7},{... | collective-permute-start | bytes 786440 | tf_op jit(solution)/shard_map/ppermute | solution.py:15
  38.2 1.3 copy-start.2
  39.7 1.1 copy-start.45
  41.4 8.0 %collective-permute-start.6 = (f32[4,1,128,128]{3,2,1,0:T(8,128)S(1)}, f32[4,1,128,128]{3,2,1,0:T(8,128)S(1)}, u32[]{:S(2)}, u32[]{:S(2)}) collective-permute-start(f32[4,1,128,128]{3,2,1,0:T(8,128)S(1)} %get-tuple-element.80), channel_id=1, source_target_pairs={{4,0},{8,4},{12,8},{5,1},{9,5},{13,9},{6,2},{10,6},{14,10},{7,3},{... | collective-permute-start | bytes 786440 | tf_op jit(solution)/shard_map/ppermute | solution.py:17
  42.8 7.6 %collective-permute-start.7 = (f32[4,1,128,128]{3,2,1,0:T(8,128)S(1)}, f32[4,1,128,128]{3,2,1,0:T(8,128)S(1)}, u32[]{:S(2)}, u32[]{:S(2)}) collective-permute-start(f32[4,1,128,128]{3,2,1,0:T(8,128)S(1)} %get-tuple-element.79), channel_id=1, source_target_pairs={{0,4},{4,8},{8,12},{1,5},{5,9},{9,13},{2,6},{6,10},{10,14},{3,7},{... | collective-permute-start | bytes 786440 | tf_op jit(solution)/shard_map/ppermute | solution.py:15
  50.8 1.0 copy-start.35
  51.8 7.1 %copy-start.9 = (f32[2,128,128]{2,1,0:T(8,128)S(1)}, f32[2,128,128]{2,1,0:T(8,128)}, u32[]{:S(2)}) copy-start(f32[2,128,128]{2,1,0:T(8,128)} %get-tuple-element.56) | copy-start | bytes 393220
  52.4 8.1 %collective-permute-start.9 = (f32[4,1,128,128]{3,2,1,0:T(8,128)S(1)}, f32[4,1,128,128]{3,2,1,0:T(8,128)S(1)}, u32[]{:S(2)}, u32[]{:S(2)}) collective-permute-start(f32[4,1,128,128]{3,2,1,0:T(8,128)S(1)} %get-tuple-element.77), channel_id=1, source_target_pairs={{0,4},{4,8},{8,12},{1,5},{5,9},{9,13},{2,6},{6,10},{10,14},{3,7},{... | collective-permute-start | bytes 786440 | tf_op jit(solution)/shard_map/ppermute | solution.py:15
  59.0 5.4 %collective-permute-start.8 = (f32[4,1,128,128]{3,2,1,0:T(8,128)S(1)}, f32[4,1,128,128]{3,2,1,0:T(8,128)S(1)}, u32[]{:S(2)}, u32[]{:S(2)}) collective-permute-start(f32[4,1,128,128]{3,2,1,0:T(8,128)S(1)} %get-tuple-element.78), channel_id=1, source_target_pairs={{4,0},{8,4},{12,8},{5,1},{9,5},{13,9},{6,2},{10,6},{14,10},{7,3},{... | collective-permute-start | bytes 786440 | tf_op jit(solution)/shard_map/ppermute | solution.py:17
  66.5 8.4 %collective-permute-start.11 = (f32[4,1,128,128]{3,2,1,0:T(8,128)S(1)}, f32[4,1,128,128]{3,2,1,0:T(8,128)S(1)}, u32[]{:S(2)}, u32[]{:S(2)}) collective-permute-start(f32[4,1,128,128]{3,2,1,0:T(8,128)S(1)} %get-tuple-element.75), channel_id=1, source_target_pairs={{0,4},{4,8},{8,12},{1,5},{5,9},{9,13},{2,6},{6,10},{10,14},{3,7},{... | collective-permute-start | bytes 786440 | tf_op jit(solution)/shard_map/ppermute | solution.py:15
  73.4 3.4 %collective-permute-start.10 = (f32[4,1,128,128]{3,2,1,0:T(8,128)S(1)}, f32[4,1,128,128]{3,2,1,0:T(8,128)S(1)}, u32[]{:S(2)}, u32[]{:S(2)}) collective-permute-start(f32[4,1,128,128]{3,2,1,0:T(8,128)S(1)} %get-tuple-element.76), channel_id=1, source_target_pairs={{4,0},{8,4},{12,8},{5,1},{9,5},{13,9},{6,2},{10,6},{14,10},{7,3},{... | collective-permute-start | bytes 786440 | tf_op jit(solution)/shard_map/ppermute | solution.py:17
  77.3 1.0 copy-start.29
  78.3 6.8 %copy-start.8 = (f32[2,128,128]{2,1,0:T(8,128)S(1)}, f32[2,128,128]{2,1,0:T(8,128)}, u32[]{:S(2)}) copy-start(f32[2,128,128]{2,1,0:T(8,128)} %copy-done.7) | copy-start | bytes 393220
  78.9 8.0 %collective-permute-start.13 = (f32[4,1,128,128]{3,2,1,0:T(8,128)S(1)}, f32[4,1,128,128]{3,2,1,0:T(8,128)S(1)}, u32[]{:S(2)}, u32[]{:S(2)}) collective-permute-start(f32[4,1,128,128]{3,2,1,0:T(8,128)S(1)} %get-tuple-element.73), channel_id=1, source_target_pairs={{0,4},{4,8},{8,12},{1,5},{5,9},{9,13},{2,6},{6,10},{10,14},{3,7},{... | collective-permute-start | bytes 786440 | tf_op jit(solution)/shard_map/ppermute | solution.py:15
  85.2 3.6 %collective-permute-start.12 = (f32[4,1,128,128]{3,2,1,0:T(8,128)S(1)}, f32[4,1,128,128]{3,2,1,0:T(8,128)S(1)}, u32[]{:S(2)}, u32[]{:S(2)}) collective-permute-start(f32[4,1,128,128]{3,2,1,0:T(8,128)S(1)} %get-tuple-element.74), channel_id=1, source_target_pairs={{4,0},{8,4},{12,8},{5,1},{9,5},{13,9},{6,2},{10,6},{14,10},{7,3},{... | collective-permute-start | bytes 786440 | tf_op jit(solution)/shard_map/ppermute | solution.py:17
  89.2 1.0 copy-start.26
  90.8 7.7 %collective-permute-start.15 = (f32[4,1,128,128]{3,2,1,0:T(8,128)S(1)}, f32[4,1,128,128]{3,2,1,0:T(8,128)S(1)}, u32[]{:S(2)}, u32[]{:S(2)}) collective-permute-start(f32[4,1,128,128]{3,2,1,0:T(8,128)S(1)} %get-tuple-element.71), channel_id=1, source_target_pairs={{0,4},{4,8},{8,12},{1,5},{5,9},{9,13},{2,6},{6,10},{10,14},{3,7},{... | collective-permute-start | bytes 786440 | tf_op jit(solution)/shard_map/ppermute | solution.py:15
  97.1 3.4 %collective-permute-start.14 = (f32[4,1,128,128]{3,2,1,0:T(8,128)S(1)}, f32[4,1,128,128]{3,2,1,0:T(8,128)S(1)}, u32[]{:S(2)}, u32[]{:S(2)}) collective-permute-start(f32[4,1,128,128]{3,2,1,0:T(8,128)S(1)} %get-tuple-element.72), channel_id=1, source_target_pairs={{4,0},{8,4},{12,8},{5,1},{9,5},{13,9},{6,2},{10,6},{14,10},{7,3},{... | collective-permute-start | bytes 786440 | tf_op jit(solution)/shard_map/ppermute | solution.py:17
  100.9 1.0 copy-start.16
  102.5 7.9 %collective-permute-start.17 = (f32[4,1,128,128]{3,2,1,0:T(8,128)S(1)}, f32[4,1,128,128]{3,2,1,0:T(8,128)S(1)}, u32[]{:S(2)}, u32[]{:S(2)}) collective-permute-start(f32[4,1,128,128]{3,2,1,0:T(8,128)S(1)} %get-tuple-element.69), channel_id=1, source_target_pairs={{0,4},{4,8},{8,12},{1,5},{5,9},{9,13},{2,6},{6,10},{10,14},{3,7},{... | collective-permute-start | bytes 786440 | tf_op jit(solution)/shard_map/ppermute | solution.py:15
  108.9 4.4 %copy-start.39 = (f32[1,2,128,128]{3,2,1,0:T(8,128)}, f32[1,2,128,128]{3,2,1,0:T(8,128)S(1)}, u32[]{:S(2)}) copy-start(f32[1,2,128,128]{3,2,1,0:T(8,128)S(1)} %get-tuple-element.189) | copy-start | bytes 393220
  108.9 4.4 %copy-start.41 = (f32[1,2,128,128]{3,2,1,0:T(8,128)}, f32[1,2,128,128]{3,2,1,0:T(8,128)S(1)}, u32[]{:S(2)}) copy-start(f32[1,2,128,128]{3,2,1,0:T(8,128)S(1)} %get-tuple-element.190) | copy-start | bytes 393220
  108.9 3.4 %collective-permute-start.16 = (f32[4,1,128,128]{3,2,1,0:T(8,128)S(1)}, f32[4,1,128,128]{3,2,1,0:T(8,128)S(1)}, u32[]{:S(2)}, u32[]{:S(2)}) collective-permute-start(f32[4,1,128,128]{3,2,1,0:T(8,128)S(1)} %get-tuple-element.70), channel_id=1, source_target_pairs={{4,0},{8,4},{12,8},{5,1},{9,5},{13,9},{6,2},{10,6},{14,10},{7,3},{... | collective-permute-start | bytes 786440 | tf_op jit(solution)/shard_map/ppermute | solution.py:17
  110.4 2.9 %copy-start.43 = (f32[1,2,128,128]{3,2,1,0:T(8,128)}, f32[1,2,128,128]{3,2,1,0:T(8,128)S(1)}, u32[]{:S(2)}) copy-start(f32[1,2,128,128]{3,2,1,0:T(8,128)S(1)} %fusion.27) | copy-start | bytes 393220
  114.4 12.7 %collective-permute-start.18 = (f32[4,2,128,128]{3,2,1,0:T(8,128)S(1)}, f32[4,2,128,128]{3,2,1,0:T(8,128)S(1)}, u32[]{:S(2)}, u32[]{:S(2)}) collective-permute-start(f32[4,2,128,128]{3,2,1,0:T(8,128)S(1)} %pad_maximum_fusion.2), channel_id=1, source_target_pairs={{0,3},{1,0},{2,1},{3,2},{4,7},{5,4},{6,5},{7,6},{8,11},{9,8},{10,9... | collective-permute-start | bytes 1572872 | tf_op jit(solution)/shard_map/ppermute | solution.py:27
  127.1 6.7 %collective-permute-start.20 = (f32[4,1,128,128]{3,2,1,0:T(8,128)S(1)}, f32[4,1,128,128]{3,2,1,0:T(8,128)S(1)}, u32[]{:S(2)}, u32[]{:S(2)}) collective-permute-start(f32[4,1,128,128]{3,2,1,0:T(8,128)S(1)} %get-tuple-element.51), channel_id=1, source_target_pairs={{0,4},{4,8},{8,12},{1,5},{5,9},{9,13},{2,6},{6,10},{10,14},{3,7},{... | collective-permute-start | bytes 786440 | tf_op jit(solution)/shard_map/ppermute | solution.py:15
  132.5 3.4 %collective-permute-start.19 = (f32[4,1,128,128]{3,2,1,0:T(8,128)S(1)}, f32[4,1,128,128]{3,2,1,0:T(8,128)S(1)}, u32[]{:S(2)}, u32[]{:S(2)}) collective-permute-start(f32[4,1,128,128]{3,2,1,0:T(8,128)S(1)} %get-tuple-element.52), channel_id=1, source_target_pairs={{4,0},{8,4},{12,8},{5,1},{9,5},{13,9},{6,2},{10,6},{14,10},{7,3},{... | collective-permute-start | bytes 786440 | tf_op jit(solution)/shard_map/ppermute | solution.py:17
  137.4 7.5 %collective-permute-start.22 = (f32[4,1,128,128]{3,2,1,0:T(8,128)S(1)}, f32[4,1,128,128]{3,2,1,0:T(8,128)S(1)}, u32[]{:S(2)}, u32[]{:S(2)}) collective-permute-start(f32[4,1,128,128]{3,2,1,0:T(8,128)S(1)} %get-tuple-element.49), channel_id=1, source_target_pairs={{0,4},{4,8},{8,12},{1,5},{5,9},{9,13},{2,6},{6,10},{10,14},{3,7},{... | collective-permute-start | bytes 786440 | tf_op jit(solution)/shard_map/ppermute | solution.py:15
  143.6 3.4 %collective-permute-start.21 = (f32[4,1,128,128]{3,2,1,0:T(8,128)S(1)}, f32[4,1,128,128]{3,2,1,0:T(8,128)S(1)}, u32[]{:S(2)}, u32[]{:S(2)}) collective-permute-start(f32[4,1,128,128]{3,2,1,0:T(8,128)S(1)} %get-tuple-element.50), channel_id=1, source_target_pairs={{4,0},{8,4},{12,8},{5,1},{9,5},{13,9},{6,2},{10,6},{14,10},{7,3},{... | collective-permute-start | bytes 786440 | tf_op jit(solution)/shard_map/ppermute | solution.py:17
  148.6 7.5 %collective-permute-start.24 = (f32[4,1,128,128]{3,2,1,0:T(8,128)S(1)}, f32[4,1,128,128]{3,2,1,0:T(8,128)S(1)}, u32[]{:S(2)}, u32[]{:S(2)}) collective-permute-start(f32[4,1,128,128]{3,2,1,0:T(8,128)S(1)} %get-tuple-element.47), channel_id=1, source_target_pairs={{0,4},{4,8},{8,12},{1,5},{5,9},{9,13},{2,6},{6,10},{10,14},{3,7},{... | collective-permute-start | bytes 786440 | tf_op jit(solution)/shard_map/ppermute | solution.py:15
  154.8 3.4 %collective-permute-start.23 = (f32[4,1,128,128]{3,2,1,0:T(8,128)S(1)}, f32[4,1,128,128]{3,2,1,0:T(8,128)S(1)}, u32[]{:S(2)}, u32[]{:S(2)}) collective-permute-start(f32[4,1,128,128]{3,2,1,0:T(8,128)S(1)} %get-tuple-element.48), channel_id=1, source_target_pairs={{4,0},{8,4},{12,8},{5,1},{9,5},{13,9},{6,2},{10,6},{14,10},{7,3},{... | collective-permute-start | bytes 786440 | tf_op jit(solution)/shard_map/ppermute | solution.py:17
  159.7 7.7 %collective-permute-start.26 = (f32[4,1,128,128]{3,2,1,0:T(8,128)S(1)}, f32[4,1,128,128]{3,2,1,0:T(8,128)S(1)}, u32[]{:S(2)}, u32[]{:S(2)}) collective-permute-start(f32[4,1,128,128]{3,2,1,0:T(8,128)S(1)} %get-tuple-element.45), channel_id=1, source_target_pairs={{0,4},{4,8},{8,12},{1,5},{5,9},{9,13},{2,6},{6,10},{10,14},{3,7},{... | collective-permute-start | bytes 786440 | tf_op jit(solution)/shard_map/ppermute | solution.py:15
  165.9 3.4 %collective-permute-start.25 = (f32[4,1,128,128]{3,2,1,0:T(8,128)S(1)}, f32[4,1,128,128]{3,2,1,0:T(8,128)S(1)}, u32[]{:S(2)}, u32[]{:S(2)}) collective-permute-start(f32[4,1,128,128]{3,2,1,0:T(8,128)S(1)} %get-tuple-element.46), channel_id=1, source_target_pairs={{4,0},{8,4},{12,8},{5,1},{9,5},{13,9},{6,2},{10,6},{14,10},{7,3},{... | collective-permute-start | bytes 786440 | tf_op jit(solution)/shard_map/ppermute | solution.py:17
  170.9 7.5 %collective-permute-start.28 = (f32[4,1,128,128]{3,2,1,0:T(8,128)S(1)}, f32[4,1,128,128]{3,2,1,0:T(8,128)S(1)}, u32[]{:S(2)}, u32[]{:S(2)}) collective-permute-start(f32[4,1,128,128]{3,2,1,0:T(8,128)S(1)} %get-tuple-element.43), channel_id=1, source_target_pairs={{0,4},{4,8},{8,12},{1,5},{5,9},{9,13},{2,6},{6,10},{10,14},{3,7},{... | collective-permute-start | bytes 786440 | tf_op jit(solution)/shard_map/ppermute | solution.py:15
  177.0 3.4 %collective-permute-start.27 = (f32[4,1,128,128]{3,2,1,0:T(8,128)S(1)}, f32[4,1,128,128]{3,2,1,0:T(8,128)S(1)}, u32[]{:S(2)}, u32[]{:S(2)}) collective-permute-start(f32[4,1,128,128]{3,2,1,0:T(8,128)S(1)} %get-tuple-element.44), channel_id=1, source_target_pairs={{4,0},{8,4},{12,8},{5,1},{9,5},{13,9},{6,2},{10,6},{14,10},{7,3},{... | collective-permute-start | bytes 786440 | tf_op jit(solution)/shard_map/ppermute | solution.py:17
  182.0 7.5 %collective-permute-start.30 = (f32[4,1,128,128]{3,2,1,0:T(8,128)S(1)}, f32[4,1,128,128]{3,2,1,0:T(8,128)S(1)}, u32[]{:S(2)}, u32[]{:S(2)}) collective-permute-start(f32[4,1,128,128]{3,2,1,0:T(8,128)S(1)} %get-tuple-element.41), channel_id=1, source_target_pairs={{0,4},{4,8},{8,12},{1,5},{5,9},{9,13},{2,6},{6,10},{10,14},{3,7},{... | collective-permute-start | bytes 786440 | tf_op jit(solution)/shard_map/ppermute | solution.py:15
  188.2 3.4 %collective-permute-start.29 = (f32[4,1,128,128]{3,2,1,0:T(8,128)S(1)}, f32[4,1,128,128]{3,2,1,0:T(8,128)S(1)}, u32[]{:S(2)}, u32[]{:S(2)}) collective-permute-start(f32[4,1,128,128]{3,2,1,0:T(8,128)S(1)} %get-tuple-element.42), channel_id=1, source_target_pairs={{4,0},{8,4},{12,8},{5,1},{9,5},{13,9},{6,2},{10,6},{14,10},{7,3},{... | collective-permute-start | bytes 786440 | tf_op jit(solution)/shard_map/ppermute | solution.py:17
  193.1 7.5 %collective-permute-start.32 = (f32[4,1,128,128]{3,2,1,0:T(8,128)S(1)}, f32[4,1,128,128]{3,2,1,0:T(8,128)S(1)}, u32[]{:S(2)}, u32[]{:S(2)}) collective-permute-start(f32[4,1,128,128]{3,2,1,0:T(8,128)S(1)} %get-tuple-element.39), channel_id=1, source_target_pairs={{0,4},{4,8},{8,12},{1,5},{5,9},{9,13},{2,6},{6,10},{10,14},{3,7},{... | collective-permute-start | bytes 786440 | tf_op jit(solution)/shard_map/ppermute | solution.py:15
  199.3 3.4 %collective-permute-start.31 = (f32[4,1,128,128]{3,2,1,0:T(8,128)S(1)}, f32[4,1,128,128]{3,2,1,0:T(8,128)S(1)}, u32[]{:S(2)}, u32[]{:S(2)}) collective-permute-start(f32[4,1,128,128]{3,2,1,0:T(8,128)S(1)} %get-tuple-element.40), channel_id=1, source_target_pairs={{4,0},{8,4},{12,8},{5,1},{9,5},{13,9},{6,2},{10,6},{14,10},{7,3},{... | collective-permute-start | bytes 786440 | tf_op jit(solution)/shard_map/ppermute | solution.py:17
  202.8 1.4 copy-start.6
  205.7 14.6 %collective-permute-start.36 = (f32[4,1,128,128]{3,2,1,0:T(8,128)S(1)}, f32[4,1,128,128]{3,2,1,0:T(8,128)S(1)}, u32[]{:S(2)}, u32[]{:S(2)}) collective-permute-start(f32[4,1,128,128]{3,2,1,0:T(8,128)S(1)} %get-tuple-element.37), channel_id=1, source_target_pairs={{0,4},{4,8},{8,12},{1,5},{5,9},{9,13},{2,6},{6,10},{10,14},{3,7},{... | collective-permute-start | bytes 786440 | tf_op jit(solution)/shard_map/ppermute | solution.py:15
  211.9 5.5 %collective-permute-start.33 = (f32[2,128,128]{2,1,0:T(8,128)S(1)}, f32[2,128,128]{2,1,0:T(8,128)S(1)}, u32[]{:S(2)}, u32[]{:S(2)}) collective-permute-start(f32[2,128,128]{2,1,0:T(8,128)S(1)} %get-tuple-element.10), channel_id=1, source_target_pairs={{0,1},{1,0},{2,3},{3,2},{4,5},{5,4},{6,7},{7,6},{8,9},{9,8},{10,11... | collective-permute-start | bytes 393224 | tf_op jit(solution)/shard_map/ppermute | solution.py:164
  212.1 8.2 %collective-permute-start.35 = (f32[4,1,128,128]{3,2,1,0:T(8,128)S(1)}, f32[4,1,128,128]{3,2,1,0:T(8,128)S(1)}, u32[]{:S(2)}, u32[]{:S(2)}) collective-permute-start(f32[4,1,128,128]{3,2,1,0:T(8,128)S(1)} %get-tuple-element.38), channel_id=1, source_target_pairs={{4,0},{8,4},{12,8},{5,1},{9,5},{13,9},{6,2},{10,6},{14,10},{7,3},{... | collective-permute-start | bytes 786440 | tf_op jit(solution)/shard_map/ppermute | solution.py:17
  217.4 8.8 %collective-permute-start.34 = (f32[2,128,128]{2,1,0:T(8,128)S(1)}, f32[2,128,128]{2,1,0:T(8,128)S(1)}, u32[]{:S(2)}, u32[]{:S(2)}) collective-permute-start(f32[2,128,128]{2,1,0:T(8,128)S(1)} %add.1312), channel_id=1, source_target_pairs={{0,2},{1,3},{2,0},{3,1},{4,6},{5,7},{6,4},{7,5},{8,10},{9,11},{10,... | collective-permute-start | bytes 393224 | tf_op jit(solution)/shard_map/ppermute | solution.py:164
  220.4 1.1 copy-start.44
  (32 other events, 30.5 us)
